TPU v7x, 512 devices: a whole 4x8x8 slice. The times are simulated.
512 devices in a mesh: seq: 32 (over x_lo, z, core), tensor: 16 (over x_hi, y).
Axes of the slice: x: 4 (x_hi: 2, x_lo: 2; x = x_hi * 2 + x_lo), y: 8, z: 8, core: 2. Of those that a mesh axis runs over, the one named last changes fastest.
Arguments:
- qkv: bfloat16 [3, 8192, 8192], P(None, 'seq', 'tensor'), may hold values from -6 to 6
- conv_weight: float32 [3, 3, 8192], P(None, None, 'tensor'), may hold values from -3.6 to 3.6
- decay_rate: float32 [16, 8192], P(None, 'tensor'), may hold values from 1e-05 to 0.06
- residue: float32 [16, 8192], P(None, 'tensor'), may hold values from -3 to 3
- skip_gain: float32 [8192], P('tensor'), may hold values from -5 to 5
- out_weight: bfloat16 [8192, 8192], P('seq', 'tensor'), may hold values from -0.125 to 0.125
Outputs:
- mixer_out: bfloat16 [8192, 8192], P('seq', 'tensor')
All inputs are finite; a program needn't handle non-finite values.
Results may differ from a plain program's by a relative error of at most 0.0049.
Values may be sent and summed in bfloat16 or wider, within the bound.
No kernel may reach another device: no remote copies, remote signals or barrier semaphores. Data moves between devices by JAX's collectives and lax.ppermute only.
A program may use at most 64 MiB of HBM per device.

v0:
```python
import jax
import jax.numpy as jnp
from jax import lax
from jax.sharding import PartitionSpec as P


KS = 3


PRECISE = lax.Precision.HIGHEST


def passed_along(block, axis, distance):
    devices = range(lax.axis_size(axis))
    route = [(i - distance, i) for i in devices if i - distance in devices]
    return lax.ppermute(block, axis, route)


def shifted(block, axis, route):
    return lax.ppermute(block, axis, route)


def ring_gather(block, axis, ring):
    size = lax.axis_size(axis)
    ring = min(ring, size)
    halves = size // ring
    place = lax.axis_index(axis)
    if halves == 2:
        partner = shifted(block, axis, [(i, i ^ ring) for i in range(size)])
        first = place // ring == 0
        chunk = jnp.where(first, jnp.stack([block, partner]), jnp.stack([partner, block]))
    else:
        chunk = block[None]
    forward = [(i, (i // ring) * ring + (i % ring + 1) % ring) for i in range(size)]
    backward = [(i, (i // ring) * ring + (i % ring - 1) % ring) for i in range(size)]
    ahead, behind = [], []
    up, down = chunk, chunk
    for step in range(ring // 2):
        up = shifted(up, axis, forward)
        behind.append(up)
        if step < (ring - 1) // 2:
            down = shifted(down, axis, backward)
            ahead.append(down)
    return [chunk] + ahead + behind[::-1]


def entering_state(local_state, rate, tokens_here, axis):
    sections = lax.axis_size(axis)
    state = jnp.zeros_like(local_state)
    for distance in range(1, min(4, sections - 1) + 1):
        lag = distance - 1
        state = state + jnp.exp(-rate * (tokens_here * lag)) * passed_along(local_state, axis, distance)
    width = 4
    while width < sections:
        grown = state
        for step in range(1, 4):
            distance = width * step
            if distance >= sections:
                break
            grown = grown + jnp.exp(-rate * (tokens_here * distance)) * passed_along(state, axis, distance)
        state = grown
        width *= 4
    return state


def body(qkv, conv_weight, decay_rate, residue, skip_gain, out_weight):
    tokens_here = qkv.shape[1]
    channels = qkv.shape[2]
    tail_rows = qkv[:, tokens_here - (KS - 1) :, :]
    previous = passed_along(tail_rows, "seq", 1)
    extended = jnp.concatenate([previous, qkv], axis=1).astype(jnp.float32)
    filtered = jnp.zeros((3, tokens_here, channels), jnp.float32)
    for offset in range(KS):
        start_row = KS - 1 - offset
        filtered = (
            filtered
            + conv_weight[:, offset, None, :] * extended[:, start_row : start_row + tokens_here, :]
        )
    product = filtered[1] * filtered[2]

    return finish(filtered, product, decay_rate, residue, skip_gain, out_weight)


def finish(filtered, product, decay_rate, residue, skip_gain, out_weight):
    tokens_here, channels = product.shape
    modes = decay_rate.shape[0]
    rate = decay_rate
    mode_weight = residue * jnp.sqrt(-jnp.expm1(-2.0 * rate))
    lags = jnp.arange(tokens_here, dtype=jnp.float32)[:, None, None]
    local_state = jnp.sum(
        jnp.exp(-rate[None] * (tokens_here - 1 - lags)) * product[:, None, :], axis=0
    )
    section_entering = entering_state(local_state, rate, tokens_here, "seq")
    growth = jnp.exp(rate[None] * lags)
    scaled = (growth * product[:, None, :]).reshape(tokens_here, modes * channels)
    lower = (jnp.arange(tokens_here)[:, None] >= jnp.arange(tokens_here)[None, :]).astype(jnp.float32)
    running = jnp.dot(lower, scaled, precision=PRECISE).reshape(tokens_here, modes, channels)
    shrink = jnp.exp(-rate[None] * lags)
    inner = jnp.sum(mode_weight[None] * shrink * running, axis=1)
    carried = jnp.sum(
        (mode_weight * section_entering)[None] * jnp.exp(-rate[None] * (lags + 1.0)), axis=1
    )
    long_part = inner + carried
    long_part = long_part + skip_gain[None, :] * product
    mixed_local = (filtered[0] * long_part).astype(jnp.bfloat16)
    features = ring_gather(mixed_local, "tensor", 8)
    weight_all = lax.all_gather(out_weight, "seq", axis=0, tiled=True)
    ring = len(features)
    halves = features[0].shape[0]
    weight_all = weight_all.reshape(halves, ring, channels, weight_all.shape[1])
    place = lax.axis_index("tensor") % ring
    projected = jnp.zeros((features[0].shape[1], weight_all.shape[-1]), jnp.float32)
    for r in range(ring):
        taken = lax.dynamic_index_in_dim(weight_all, (place + r) % ring, 1, False)
        projected = projected + jnp.einsum(
            "htc,hco->to", features[r], taken, preferred_element_type=jnp.float32
        )
    return projected.astype(jnp.bfloat16)


def solution(mesh):
    return jax.shard_map(
        body,
        mesh=mesh,
        in_specs=(
            P(None, "seq", "tensor"),
            P(None, None, "tensor"),
            P(None, "tensor"),
            P(None, "tensor"),
            P("tensor"),
            P("seq", "tensor"),
        ),
        out_specs=P("seq", "tensor"),
        check_vma=False,
    )
```

profile of v0, /device:TPU:26, one launch (start us, length us, event | category | flops | bytes accessed | tf_op | source)
XLA Modules:
  0.0 150.4 jit_solution(12729208313366775348)
XLA Ops:
  11.6 8.1 %collective-permute-done = bf16[3,2,512]{2,1,0:T(2,128)(2,1)S(1)} collective-permute-done((bf16[3,2,512]{2,1,0:T(2,128)(2,1)S(1)}, bf16[3,2,512]{2,1,0:T(2,128)(2,1)S(1)}, u32[]{:S(2)}, u32[]{:S(2)}) %collective-permute-start) | collective-permute-done | bytes 6176 | tf_op jit(solution)/shard_map/ppermute | solution.py:16
  23.1 1.9 %collective-permute-start.1 = (f32[16,512]{1,0:T(8,128)S(1)}, f32[16,512]{1,0:T(8,128)S(1)}, u32[]{:S(2)}, u32[]{:S(2)}) collective-permute-start(f32[16,512]{1,0:T(8,128)S(1)} %multiply_reduce_fusion.1), channel_id=1, source_target_pairs={{0,16},{16,32},{32,48},{48,64},{64,80},{80,96},{96,112},{112,128},... | collective-permute-start | bytes 98312 | tf_op jit(solution)/shard_map/ppermute | solution.py:16
  25.0 1.9 %collective-permute-start.2 = (f32[16,512]{1,0:T(8,128)S(1)}, f32[16,512]{1,0:T(8,128)S(1)}, u32[]{:S(2)}, u32[]{:S(2)}) collective-permute-start(f32[16,512]{1,0:T(8,128)S(1)} %multiply_reduce_fusion.1), channel_id=1, source_target_pairs={{0,32},{16,48},{32,64},{48,80},{64,96},{80,112},{96,128},{112,144}... | collective-permute-start | bytes 98312 | tf_op jit(solution)/shard_map/ppermute | solution.py:16
  27.0 1.9 %collective-permute-start.3 = (f32[16,512]{1,0:T(8,128)S(1)}, f32[16,512]{1,0:T(8,128)S(1)}, u32[]{:S(2)}, u32[]{:S(2)}) collective-permute-start(f32[16,512]{1,0:T(8,128)S(1)} %multiply_reduce_fusion.1), channel_id=1, source_target_pairs={{0,48},{16,64},{32,80},{48,96},{64,112},{80,128},{96,144},{112,160... | collective-permute-start | bytes 98312 | tf_op jit(solution)/shard_map/ppermute | solution.py:16
  28.9 6.2 %collective-permute-start.4 = (f32[16,512]{1,0:T(8,128)S(1)}, f32[16,512]{1,0:T(8,128)S(1)}, u32[]{:S(2)}, u32[]{:S(2)}) collective-permute-start(f32[16,512]{1,0:T(8,128)S(1)} %multiply_reduce_fusion.1), channel_id=1, source_target_pairs={{0,64},{16,80},{32,96},{48,112},{64,128},{80,144},{96,160},{112,17... | collective-permute-start | bytes 98312 | tf_op jit(solution)/shard_map/ppermute | solution.py:16
  36.4 2.8 %collective-permute-done.4 = f32[16,512]{1,0:T(8,128)S(1)} collective-permute-done((f32[16,512]{1,0:T(8,128)S(1)}, f32[16,512]{1,0:T(8,128)S(1)}, u32[]{:S(2)}, u32[]{:S(2)}) %collective-permute-start.4) | collective-permute-done | bytes 32800 | tf_op jit(solution)/shard_map/ppermute | solution.py:16
  39.3 3.2 %collective-permute-start.5 = (f32[16,512]{1,0:T(8,128)S(1)}, f32[16,512]{1,0:T(8,128)S(1)}, u32[]{:S(2)}, u32[]{:S(2)}) collective-permute-start(f32[16,512]{1,0:T(8,128)S(1)} %multiply_add_fusion.1), channel_id=1, source_target_pairs={{0,64},{16,80},{32,96},{48,112},{64,128},{80,144},{96,160},{112,17... | collective-permute-start | bytes 98312 | tf_op jit(solution)/shard_map/ppermute | solution.py:16
  42.5 5.8 %collective-permute-start.6 = (f32[16,512]{1,0:T(8,128)S(1)}, f32[16,512]{1,0:T(8,128)S(1)}, u32[]{:S(2)}, u32[]{:S(2)}) collective-permute-start(f32[16,512]{1,0:T(8,128)S(1)} %multiply_add_fusion.1), channel_id=1, source_target_pairs={{0,128},{16,144},{32,160},{48,176},{64,192},{80,208},{96,224},{112... | collective-permute-start | bytes 98312 | tf_op jit(solution)/shard_map/ppermute | solution.py:16
  50.2 3.6 %collective-permute-done.6 = f32[16,512]{1,0:T(8,128)S(1)} collective-permute-done((f32[16,512]{1,0:T(8,128)S(1)}, f32[16,512]{1,0:T(8,128)S(1)}, u32[]{:S(2)}, u32[]{:S(2)}) %collective-permute-start.6) | collective-permute-done | bytes 32800 | tf_op jit(solution)/shard_map/ppermute | solution.py:16
  53.9 3.4 %collective-permute-done.7 = f32[16,512]{1,0:T(8,128)S(1)} collective-permute-done((f32[16,512]{1,0:T(8,128)S(1)}, f32[16,512]{1,0:T(8,128)S(1)}, u32[]{:S(2)}, u32[]{:S(2)}) %collective-permute-start.7) | collective-permute-done | bytes 32800 | tf_op jit(solution)/shard_map/ppermute | solution.py:16
  60.2 3.6 %collective-permute-done.8 = f32[16,512]{1,0:T(8,128)S(1)} collective-permute-done((f32[16,512]{1,0:T(8,128)S(1)}, f32[16,512]{1,0:T(8,128)S(1)}, u32[]{:S(2)}, u32[]{:S(2)}) %collective-permute-start.8) | collective-permute-done | bytes 32800 | tf_op jit(solution)/shard_map/ppermute | solution.py:16
  65.2 6.5 %multiply_reduce_fusion.2 = f32[256,512]{1,0:T(8,128)S(1)} fusion(f32[16,512]{1,0:T(8,128)S(1)} %neg.6, f32[16,512]{1,0:T(8,128)S(1)} %get-tuple-element.6, f32[16,512,256]{2,1,0:T(8,128)S(1)} %bitcast.122), kind=kOutput, calls=%fused_computation.3 | convolution fusion | flops 6450774016 | bytes 8978432 | tf_op jit(solution)/shard_map/dot_general | solution.py:97
  72.1 3.8 %collective-permute-start.9 = (bf16[256,512]{1,0:T(8,128)(2,1)S(1)}, bf16[256,512]{1,0:T(8,128)(2,1)S(1)}, u32[]{:S(2)}, u32[]{:S(2)}) collective-permute-start(bf16[256,512]{1,0:T(8,128)(2,1)S(1)} %fusion.26), channel_id=1, source_target_pairs={{0,8},{1,9},{2,10},{3,11},{4,12},{5,13},{6,14},{7,15},{8,0},{9,1},... | collective-permute-start | bytes 786440 | tf_op jit(solution)/shard_map/ppermute | solution.py:20
  76.2 12.0 %collective-permute-done.9 = bf16[256,512]{1,0:T(8,128)(2,1)S(1)} collective-permute-done((bf16[256,512]{1,0:T(8,128)(2,1)S(1)}, bf16[256,512]{1,0:T(8,128)(2,1)S(1)}, u32[]{:S(2)}, u32[]{:S(2)}) %collective-permute-start.9) | collective-permute-done | bytes 262176 | tf_op jit(solution)/shard_map/ppermute | solution.py:20
  88.3 4.2 %collective-permute-start.13 = (bf16[2,256,512]{2,1,0:T(8,128)(2,1)S(1)}, bf16[2,256,512]{2,1,0:T(8,128)(2,1)S(1)}, u32[]{:S(2)}, u32[]{:S(2)}) collective-permute-start(bf16[2,256,512]{2,1,0:T(8,128)(2,1)S(1)} %maximum_select_fusion), channel_id=1, source_target_pairs={{0,1},{1,2},{2,3},{3,4},{4,5},{5,6},{6,7},{7,0},{8,9},{9,10},{10,1... | collective-permute-start | bytes 1572872 | tf_op jit(solution)/shard_map/ppermute | solution.py:20
  94.4 6.1 %collective-permute-done.13 = bf16[2,256,512]{2,1,0:T(8,128)(2,1)S(1)} collective-permute-done((bf16[2,256,512]{2,1,0:T(8,128)(2,1)S(1)}, bf16[2,256,512]{2,1,0:T(8,128)(2,1)S(1)}, u32[]{:S(2)}, u32[]{:S(2)}) %collective-permute-start.13) | collective-permute-done | bytes 524320 | tf_op jit(solution)/shard_map/ppermute | solution.py:20
  100.6 5.6 %collective-permute-start.14 = (bf16[2,256,512]{2,1,0:T(8,128)(2,1)S(1)}, bf16[2,256,512]{2,1,0:T(8,128)(2,1)S(1)}, u32[]{:S(2)}, u32[]{:S(2)}) collective-permute-start(bf16[2,256,512]{2,1,0:T(8,128)(2,1)S(1)} %collective-permute-done.13), channel_id=1, source_target_pairs={{0,1},{1,2},{2,3},{3,4},{4,5},{5,6},{6,7},{7,0},{8,9},{9,10},{10,1... | collective-permute-start | bytes 1572872 | tf_op jit(solution)/shard_map/ppermute | solution.py:20
  106.2 1.9 %collective-permute-start.11 = (bf16[2,256,512]{2,1,0:T(8,128)(2,1)S(1)}, bf16[2,256,512]{2,1,0:T(8,128)(2,1)}, u32[]{:S(2)}, u32[]{:S(2)}) collective-permute-start(bf16[2,256,512]{2,1,0:T(8,128)(2,1)S(1)} %collective-permute-done.10), channel_id=1, source_target_pairs={{0,7},{1,0},{2,1},{3,2},{4,3},{5,4},{6,5},{7,6},{8,15},{9,8},{10,9... | collective-permute-start | bytes 1572872 | tf_op jit(solution)/shard_map/ppermute | solution.py:20
  108.1 5.3 %collective-permute-done.14 = bf16[2,256,512]{2,1,0:T(8,128)(2,1)S(1)} collective-permute-done((bf16[2,256,512]{2,1,0:T(8,128)(2,1)S(1)}, bf16[2,256,512]{2,1,0:T(8,128)(2,1)S(1)}, u32[]{:S(2)}, u32[]{:S(2)}) %collective-permute-start.14) | collective-permute-done | bytes 524320 | tf_op jit(solution)/shard_map/ppermute | solution.py:20
  113.4 5.6 %collective-permute-start.15 = (bf16[2,256,512]{2,1,0:T(8,128)(2,1)S(1)}, bf16[2,256,512]{2,1,0:T(8,128)(2,1)S(1)}, u32[]{:S(2)}, u32[]{:S(2)}) collective-permute-start(bf16[2,256,512]{2,1,0:T(8,128)(2,1)S(1)} %collective-permute-done.14), channel_id=1, source_target_pairs={{0,1},{1,2},{2,3},{3,4},{4,5},{5,6},{6,7},{7,0},{8,9},{9,10},{10,1... | collective-permute-start | bytes 1572872 | tf_op jit(solution)/shard_map/ppermute | solution.py:20
  119.1 1.9 %collective-permute-start.12 = (bf16[2,256,512]{2,1,0:T(8,128)(2,1)}, bf16[2,256,512]{2,1,0:T(8,128)(2,1)}, u32[]{:S(2)}, u32[]{:S(2)}) collective-permute-start(bf16[2,256,512]{2,1,0:T(8,128)(2,1)} %collective-permute-done.11), channel_id=1, source_target_pairs={{0,7},{1,0},{2,1},{3,2},{4,3},{5,4},{6,5},{7,6},{8,15},{9,8},{10,9... | collective-permute-start | bytes 1572872 | tf_op jit(solution)/shard_map/ppermute | solution.py:20
  121.1 5.0 %collective-permute-done.15 = bf16[2,256,512]{2,1,0:T(8,128)(2,1)S(1)} collective-permute-done((bf16[2,256,512]{2,1,0:T(8,128)(2,1)S(1)}, bf16[2,256,512]{2,1,0:T(8,128)(2,1)S(1)}, u32[]{:S(2)}, u32[]{:S(2)}) %collective-permute-start.15) | collective-permute-done | bytes 524320 | tf_op jit(solution)/shard_map/ppermute | solution.py:20
  126.1 5.6 %collective-permute-start.16 = (bf16[2,256,512]{2,1,0:T(8,128)(2,1)S(1)}, bf16[2,256,512]{2,1,0:T(8,128)(2,1)S(1)}, u32[]{:S(2)}, u32[]{:S(2)}) collective-permute-start(bf16[2,256,512]{2,1,0:T(8,128)(2,1)S(1)} %collective-permute-done.15), channel_id=1, source_target_pairs={{0,1},{1,2},{2,3},{3,4},{4,5},{5,6},{6,7},{7,0},{8,9},{9,10},{10,1... | collective-permute-start | bytes 1572872 | tf_op jit(solution)/shard_map/ppermute | solution.py:20
  133.5 2.1 %convolution_bitcast_fusion.2 = f32[256,512]{1,0:T(8,128)S(1)} fusion(bf16[2,256,512]{2,1,0:T(8,128)(2,1)S(1)} %collective-permute-done.15, bf16[2,8,512,512]{3,2,1,0:T(8,128)(2,1)} %bitcast.115, s32[]{:T(128)S(6)} %select_n.91), kind=kOutput, calls=%fused_computation.11 | convolution fusion | flops 268435456 | bytes 2097156 | tf_op jit(solution)/shard_map/htc,hco->to/dot_general | solution.py:115
  (51 shorter events, 28.3 us)
Async XLA Ops:
  6.5 32.7 %copy-start.1 = (f32[16,512]{1,0:T(8,128)S(1)}, f32[16,512]{1,0:T(8,128)}, u32[]{:S(2)}) copy-start(f32[16,512]{1,0:T(8,128)} %param.8) | copy-start | bytes 98308
  6.5 125.2 %all-gather.2.cloned.1.call-start = ((), (), s32[]{:S(2)}) async-start(), calls=%async_computation | async-start | bytes 8650752 | tf_op jit(solution)/shard_map/all_gather | solution.py:107
  8.0 11.7 %collective-permute-start = (bf16[3,2,512]{2,1,0:T(2,128)(2,1)S(1)}, bf16[3,2,512]{2,1,0:T(2,128)(2,1)S(1)}, u32[]{:S(2)}, u32[]{:S(2)}) collective-permute-start(bf16[3,2,512]{2,1,0:T(2,128)(2,1)S(1)} %slice.31), channel_id=1, source_target_pairs={{0,16},{16,32},{32,48},{48,64},{64,80},{80,96},{96,112},{112,128},... | collective-permute-start | bytes 18440 | tf_op jit(solution)/shard_map/ppermute | solution.py:16
  21.5 42.2 %copy-start.2 = (f32[16,512]{1,0:T(8,128)S(1)}, f32[16,512]{1,0:T(8,128)}, u32[]{:S(2)}) copy-start(f32[16,512]{1,0:T(8,128)} %param.9) | copy-start | bytes 98308
  23.1 12.0 %collective-permute-start.1 = (f32[16,512]{1,0:T(8,128)S(1)}, f32[16,512]{1,0:T(8,128)S(1)}, u32[]{:S(2)}, u32[]{:S(2)}) collective-permute-start(f32[16,512]{1,0:T(8,128)S(1)} %multiply_reduce_fusion.1), channel_id=1, source_target_pairs={{0,16},{16,32},{32,48},{48,64},{64,80},{80,96},{96,112},{112,128},... | collective-permute-start | bytes 98312 | tf_op jit(solution)/shard_map/ppermute | solution.py:16
  25.0 10.1 %collective-permute-start.2 = (f32[16,512]{1,0:T(8,128)S(1)}, f32[16,512]{1,0:T(8,128)S(1)}, u32[]{:S(2)}, u32[]{:S(2)}) collective-permute-start(f32[16,512]{1,0:T(8,128)S(1)} %multiply_reduce_fusion.1), channel_id=1, source_target_pairs={{0,32},{16,48},{32,64},{48,80},{64,96},{80,112},{96,128},{112,144}... | collective-permute-start | bytes 98312 | tf_op jit(solution)/shard_map/ppermute | solution.py:16
  27.0 9.4 %collective-permute-start.3 = (f32[16,512]{1,0:T(8,128)S(1)}, f32[16,512]{1,0:T(8,128)S(1)}, u32[]{:S(2)}, u32[]{:S(2)}) collective-permute-start(f32[16,512]{1,0:T(8,128)S(1)} %multiply_reduce_fusion.1), channel_id=1, source_target_pairs={{0,48},{16,64},{32,80},{48,96},{64,112},{80,128},{96,144},{112,160... | collective-permute-start | bytes 98312 | tf_op jit(solution)/shard_map/ppermute | solution.py:16
  28.9 10.3 %collective-permute-start.4 = (f32[16,512]{1,0:T(8,128)S(1)}, f32[16,512]{1,0:T(8,128)S(1)}, u32[]{:S(2)}, u32[]{:S(2)}) collective-permute-start(f32[16,512]{1,0:T(8,128)S(1)} %multiply_reduce_fusion.1), channel_id=1, source_target_pairs={{0,64},{16,80},{32,96},{48,112},{64,128},{80,144},{96,160},{112,17... | collective-permute-start | bytes 98312 | tf_op jit(solution)/shard_map/ppermute | solution.py:16
  39.3 10.9 %collective-permute-start.5 = (f32[16,512]{1,0:T(8,128)S(1)}, f32[16,512]{1,0:T(8,128)S(1)}, u32[]{:S(2)}, u32[]{:S(2)}) collective-permute-start(f32[16,512]{1,0:T(8,128)S(1)} %multiply_add_fusion.1), channel_id=1, source_target_pairs={{0,64},{16,80},{32,96},{48,112},{64,128},{80,144},{96,160},{112,17... | collective-permute-start | bytes 98312 | tf_op jit(solution)/shard_map/ppermute | solution.py:16
  42.5 11.4 %collective-permute-start.6 = (f32[16,512]{1,0:T(8,128)S(1)}, f32[16,512]{1,0:T(8,128)S(1)}, u32[]{:S(2)}, u32[]{:S(2)}) collective-permute-start(f32[16,512]{1,0:T(8,128)S(1)} %multiply_add_fusion.1), channel_id=1, source_target_pairs={{0,128},{16,144},{32,160},{48,176},{64,192},{80,208},{96,224},{112... | collective-permute-start | bytes 98312 | tf_op jit(solution)/shard_map/ppermute | solution.py:16
  48.3 9.0 %collective-permute-start.7 = (f32[16,512]{1,0:T(8,128)S(1)}, f32[16,512]{1,0:T(8,128)S(1)}, u32[]{:S(2)}, u32[]{:S(2)}) collective-permute-start(f32[16,512]{1,0:T(8,128)S(1)} %multiply_add_fusion.1), channel_id=1, source_target_pairs={{0,192},{16,208},{32,224},{48,240},{64,256},{80,272},{96,288},{112... | collective-permute-start | bytes 98312 | tf_op jit(solution)/shard_map/ppermute | solution.py:16
  57.3 6.4 %collective-permute-start.8 = (f32[16,512]{1,0:T(8,128)S(1)}, f32[16,512]{1,0:T(8,128)S(1)}, u32[]{:S(2)}, u32[]{:S(2)}) collective-permute-start(f32[16,512]{1,0:T(8,128)S(1)} %multiply_add_fusion), channel_id=1, source_target_pairs={{0,256},{16,272},{32,288},{48,304},{64,320},{80,336},{96,352},{112... | collective-permute-start | bytes 98312 | tf_op jit(solution)/shard_map/ppermute | solution.py:16
  60.2 11.6 %copy-start.3 = (f32[512]{0:T(512)S(1)}, f32[512]{0:T(512)}, u32[]{:S(2)}) copy-start(f32[512]{0:T(512)} %param.10) | copy-start | bytes 6148
  72.1 16.1 %collective-permute-start.9 = (bf16[256,512]{1,0:T(8,128)(2,1)S(1)}, bf16[256,512]{1,0:T(8,128)(2,1)S(1)}, u32[]{:S(2)}, u32[]{:S(2)}) collective-permute-start(bf16[256,512]{1,0:T(8,128)(2,1)S(1)} %fusion.26), channel_id=1, source_target_pairs={{0,8},{1,9},{2,10},{3,11},{4,12},{5,13},{6,14},{7,15},{8,0},{9,1},... | collective-permute-start | bytes 786440 | tf_op jit(solution)/shard_map/ppermute | solution.py:20
  88.3 12.2 %collective-permute-start.13 = (bf16[2,256,512]{2,1,0:T(8,128)(2,1)S(1)}, bf16[2,256,512]{2,1,0:T(8,128)(2,1)S(1)}, u32[]{:S(2)}, u32[]{:S(2)}) collective-permute-start(bf16[2,256,512]{2,1,0:T(8,128)(2,1)S(1)} %maximum_select_fusion), channel_id=1, source_target_pairs={{0,1},{1,2},{2,3},{3,4},{4,5},{5,6},{6,7},{7,0},{8,9},{9,10},{10,1... | collective-permute-start | bytes 1572872 | tf_op jit(solution)/shard_map/ppermute | solution.py:20
  92.5 13.7 %collective-permute-start.10 = (bf16[2,256,512]{2,1,0:T(8,128)(2,1)S(1)}, bf16[2,256,512]{2,1,0:T(8,128)(2,1)S(1)}, u32[]{:S(2)}, u32[]{:S(2)}) collective-permute-start(bf16[2,256,512]{2,1,0:T(8,128)(2,1)S(1)} %maximum_select_fusion), channel_id=1, source_target_pairs={{0,7},{1,0},{2,1},{3,2},{4,3},{5,4},{6,5},{7,6},{8,15},{9,8},{10,9... | collective-permute-start | bytes 1572872 | tf_op jit(solution)/shard_map/ppermute | solution.py:20
  100.6 12.8 %collective-permute-start.14 = (bf16[2,256,512]{2,1,0:T(8,128)(2,1)S(1)}, bf16[2,256,512]{2,1,0:T(8,128)(2,1)S(1)}, u32[]{:S(2)}, u32[]{:S(2)}) collective-permute-start(bf16[2,256,512]{2,1,0:T(8,128)(2,1)S(1)} %collective-permute-done.13), channel_id=1, source_target_pairs={{0,1},{1,2},{2,3},{3,4},{4,5},{5,6},{6,7},{7,0},{8,9},{9,10},{10,1... | collective-permute-start | bytes 1572872 | tf_op jit(solution)/shard_map/ppermute | solution.py:20
  106.2 13.0 %collective-permute-start.11 = (bf16[2,256,512]{2,1,0:T(8,128)(2,1)S(1)}, bf16[2,256,512]{2,1,0:T(8,128)(2,1)}, u32[]{:S(2)}, u32[]{:S(2)}) collective-permute-start(bf16[2,256,512]{2,1,0:T(8,128)(2,1)S(1)} %collective-permute-done.10), channel_id=1, source_target_pairs={{0,7},{1,0},{2,1},{3,2},{4,3},{5,4},{6,5},{7,6},{8,15},{9,8},{10,9... | collective-permute-start | bytes 1572872 | tf_op jit(solution)/shard_map/ppermute | solution.py:20
  113.4 12.7 %collective-permute-start.15 = (bf16[2,256,512]{2,1,0:T(8,128)(2,1)S(1)}, bf16[2,256,512]{2,1,0:T(8,128)(2,1)S(1)}, u32[]{:S(2)}, u32[]{:S(2)}) collective-permute-start(bf16[2,256,512]{2,1,0:T(8,128)(2,1)S(1)} %collective-permute-done.14), channel_id=1, source_target_pairs={{0,1},{1,2},{2,3},{3,4},{4,5},{5,6},{6,7},{7,0},{8,9},{9,10},{10,1... | collective-permute-start | bytes 1572872 | tf_op jit(solution)/shard_map/ppermute | solution.py:20
  119.1 21.8 %collective-permute-start.12 = (bf16[2,256,512]{2,1,0:T(8,128)(2,1)}, bf16[2,256,512]{2,1,0:T(8,128)(2,1)}, u32[]{:S(2)}, u32[]{:S(2)}) collective-permute-start(bf16[2,256,512]{2,1,0:T(8,128)(2,1)} %collective-permute-done.11), channel_id=1, source_target_pairs={{0,7},{1,0},{2,1},{3,2},{4,3},{5,4},{6,5},{7,6},{8,15},{9,8},{10,9... | collective-permute-start | bytes 1572872 | tf_op jit(solution)/shard_map/ppermute | solution.py:20
  126.1 16.3 %collective-permute-start.16 = (bf16[2,256,512]{2,1,0:T(8,128)(2,1)S(1)}, bf16[2,256,512]{2,1,0:T(8,128)(2,1)S(1)}, u32[]{:S(2)}, u32[]{:S(2)}) collective-permute-start(bf16[2,256,512]{2,1,0:T(8,128)(2,1)S(1)} %collective-permute-done.15), channel_id=1, source_target_pairs={{0,1},{1,2},{2,3},{3,4},{4,5},{5,6},{6,7},{7,0},{8,9},{9,10},{10,1... | collective-permute-start | bytes 1572872 | tf_op jit(solution)/shard_map/ppermute | solution.py:20
  131.7 7.2 %copy-start = (bf16[8192,512]{1,0:T(8,128)(2,1)S(1)}, bf16[8192,512]{1,0:T(8,128)(2,1)}, u32[]{:S(2)}) copy-start(bf16[8192,512]{1,0:T(8,128)(2,1)} %all-gather.2.cloned.1.call-done) | copy-start | bytes 25165828
Sparse Core Ops, SparseCore 0:
  9.5 83.6 all-gather.1
where the time goes:
time: 151 us; the launch traced here: 150 us
  starting transfers between devices  56.6 us (37%)
  waiting for transfers between devices  52 us (34%)
  matrix products  18.3 us (12%)
  between operations  14 us (9%)
  other arithmetic  7.66 us (5%)
  local copies, waits for them, and re-layouts  1.86 us (1%)
    ppermute x8, starting transfers between devices, shifted(): return lax.ppermute(block, axis, route)  30.5 us
    ppermute x8, waiting for transfers between devices, shifted(): return lax.ppermute(block, axis, route)  28.4 us
    ppermute x9, starting transfers between devices, passed_along(): return lax.ppermute(block, axis, route)  26.1 us
    ppermute x9, waiting for transfers between devices, passed_along(): return lax.ppermute(block, axis, route)  22.8 us
    dot_general x8, matrix products, finish(): jnp.einsum('htc,hco->to', features[r], taken, preferred_element_type=jnp....  11.8 us
    dot_general x1, matrix products, finish(): jnp.dot(lower, scaled, precision=PRECISE)  6.55 us
  transfers between devices with their start and end apart: 18, of which 10 were waited for; matrix products, arithmetic and copies ran while one was open for 18% of the time, Pallas kernels for 0%

commit v1 on v0

--- a/solution.py
+++ b/solution.py
@@ -78,10 +78,11 @@
         )
     product = filtered[1] * filtered[2]
 
-    return finish(filtered, product, decay_rate, residue, skip_gain, out_weight)
+    mixed_local = finish(filtered, product, decay_rate, residue, skip_gain)
+    return tail(mixed_local, out_weight)
 
 
-def finish(filtered, product, decay_rate, residue, skip_gain, out_weight):
+def finish(filtered, product, decay_rate, residue, skip_gain):
     tokens_here, channels = product.shape
     modes = decay_rate.shape[0]
     rate = decay_rate
@@ -102,7 +103,11 @@
     )
     long_part = inner + carried
     long_part = long_part + skip_gain[None, :] * product
-    mixed_local = (filtered[0] * long_part).astype(jnp.bfloat16)
+    return (filtered[0] * long_part).astype(jnp.bfloat16)
+
+
+def tail(mixed_local, out_weight):
+    channels = mixed_local.shape[1]
     features = ring_gather(mixed_local, "tensor", 8)
     weight_all = lax.all_gather(out_weight, "seq", axis=0, tiled=True)
     ring = len(features)

time: 151 us -> 151 us (level)
  no operation moved by 1% of the time
where the time goes in v1:
time: 151 us; the launch traced here: 150 us
  starting transfers between devices  56.6 us (37%)
  waiting for transfers between devices  52 us (34%)
  matrix products  18.3 us (12%)
  between operations  14 us (9%)
  other arithmetic  7.66 us (5%)
  local copies, waits for them, and re-layouts  1.86 us (1%)
    ppermute x8, starting transfers between devices, shifted(): return lax.ppermute(block, axis, route)  30.5 us
    ppermute x8, waiting for transfers between devices, shifted(): return lax.ppermute(block, axis, route)  28.4 us
    ppermute x9, starting transfers between devices, passed_along(): return lax.ppermute(block, axis, route)  26.1 us
    ppermute x9, waiting for transfers between devices, passed_along(): return lax.ppermute(block, axis, route)  22.8 us
    dot_general x8, matrix products, tail(): jnp.einsum('htc,hco->to', features[r], taken, preferred_element_type=jnp....  11.8 us
    dot_general x1, matrix products, finish(): jnp.dot(lower, scaled, precision=PRECISE)  6.55 us
  transfers between devices with their start and end apart: 18, of which 10 were waited for; matrix products, arithmetic and copies ran while one was open for 18% of the time, Pallas kernels for 0%

profile of v1, /device:TPU:26, one launch (start us, length us, event | category | flops | bytes accessed | tf_op | source)
XLA Modules:
  0.0 150.4 jit_solution(12729208313366775348)
XLA Ops:
  11.6 8.1 %collective-permute-done = bf16[3,2,512]{2,1,0:T(2,128)(2,1)S(1)} collective-permute-done((bf16[3,2,512]{2,1,0:T(2,128)(2,1)S(1)}, bf16[3,2,512]{2,1,0:T(2,128)(2,1)S(1)}, u32[]{:S(2)}, u32[]{:S(2)}) %collective-permute-start) | collective-permute-done | bytes 6176 | tf_op jit(solution)/shard_map/ppermute | solution.py:16
  23.1 1.9 %collective-permute-start.1 = (f32[16,512]{1,0:T(8,128)S(1)}, f32[16,512]{1,0:T(8,128)S(1)}, u32[]{:S(2)}, u32[]{:S(2)}) collective-permute-start(f32[16,512]{1,0:T(8,128)S(1)} %multiply_reduce_fusion.1), channel_id=1, source_target_pairs={{0,16},{16,32},{32,48},{48,64},{64,80},{80,96},{96,112},{112,128},... | collective-permute-start | bytes 98312 | tf_op jit(solution)/shard_map/ppermute | solution.py:16
  25.0 1.9 %collective-permute-start.2 = (f32[16,512]{1,0:T(8,128)S(1)}, f32[16,512]{1,0:T(8,128)S(1)}, u32[]{:S(2)}, u32[]{:S(2)}) collective-permute-start(f32[16,512]{1,0:T(8,128)S(1)} %multiply_reduce_fusion.1), channel_id=1, source_target_pairs={{0,32},{16,48},{32,64},{48,80},{64,96},{80,112},{96,128},{112,144}... | collective-permute-start | bytes 98312 | tf_op jit(solution)/shard_map/ppermute | solution.py:16
  27.0 1.9 %collective-permute-start.3 = (f32[16,512]{1,0:T(8,128)S(1)}, f32[16,512]{1,0:T(8,128)S(1)}, u32[]{:S(2)}, u32[]{:S(2)}) collective-permute-start(f32[16,512]{1,0:T(8,128)S(1)} %multiply_reduce_fusion.1), channel_id=1, source_target_pairs={{0,48},{16,64},{32,80},{48,96},{64,112},{80,128},{96,144},{112,160... | collective-permute-start | bytes 98312 | tf_op jit(solution)/shard_map/ppermute | solution.py:16
  28.9 6.2 %collective-permute-start.4 = (f32[16,512]{1,0:T(8,128)S(1)}, f32[16,512]{1,0:T(8,128)S(1)}, u32[]{:S(2)}, u32[]{:S(2)}) collective-permute-start(f32[16,512]{1,0:T(8,128)S(1)} %multiply_reduce_fusion.1), channel_id=1, source_target_pairs={{0,64},{16,80},{32,96},{48,112},{64,128},{80,144},{96,160},{112,17... | collective-permute-start | bytes 98312 | tf_op jit(solution)/shard_map/ppermute | solution.py:16
  36.4 2.8 %collective-permute-done.4 = f32[16,512]{1,0:T(8,128)S(1)} collective-permute-done((f32[16,512]{1,0:T(8,128)S(1)}, f32[16,512]{1,0:T(8,128)S(1)}, u32[]{:S(2)}, u32[]{:S(2)}) %collective-permute-start.4) | collective-permute-done | bytes 32800 | tf_op jit(solution)/shard_map/ppermute | solution.py:16
  39.3 3.2 %collective-permute-start.5 = (f32[16,512]{1,0:T(8,128)S(1)}, f32[16,512]{1,0:T(8,128)S(1)}, u32[]{:S(2)}, u32[]{:S(2)}) collective-permute-start(f32[16,512]{1,0:T(8,128)S(1)} %multiply_add_fusion.1), channel_id=1, source_target_pairs={{0,64},{16,80},{32,96},{48,112},{64,128},{80,144},{96,160},{112,17... | collective-permute-start | bytes 98312 | tf_op jit(solution)/shard_map/ppermute | solution.py:16
  42.5 5.8 %collective-permute-start.6 = (f32[16,512]{1,0:T(8,128)S(1)}, f32[16,512]{1,0:T(8,128)S(1)}, u32[]{:S(2)}, u32[]{:S(2)}) collective-permute-start(f32[16,512]{1,0:T(8,128)S(1)} %multiply_add_fusion.1), channel_id=1, source_target_pairs={{0,128},{16,144},{32,160},{48,176},{64,192},{80,208},{96,224},{112... | collective-permute-start | bytes 98312 | tf_op jit(solution)/shard_map/ppermute | solution.py:16
  50.2 3.6 %collective-permute-done.6 = f32[16,512]{1,0:T(8,128)S(1)} collective-permute-done((f32[16,512]{1,0:T(8,128)S(1)}, f32[16,512]{1,0:T(8,128)S(1)}, u32[]{:S(2)}, u32[]{:S(2)}) %collective-permute-start.6) | collective-permute-done | bytes 32800 | tf_op jit(solution)/shard_map/ppermute | solution.py:16
  53.9 3.4 %collective-permute-done.7 = f32[16,512]{1,0:T(8,128)S(1)} collective-permute-done((f32[16,512]{1,0:T(8,128)S(1)}, f32[16,512]{1,0:T(8,128)S(1)}, u32[]{:S(2)}, u32[]{:S(2)}) %collective-permute-start.7) | collective-permute-done | bytes 32800 | tf_op jit(solution)/shard_map/ppermute | solution.py:16
  60.2 3.6 %collective-permute-done.8 = f32[16,512]{1,0:T(8,128)S(1)} collective-permute-done((f32[16,512]{1,0:T(8,128)S(1)}, f32[16,512]{1,0:T(8,128)S(1)}, u32[]{:S(2)}, u32[]{:S(2)}) %collective-permute-start.8) | collective-permute-done | bytes 32800 | tf_op jit(solution)/shard_map/ppermute | solution.py:16
  65.2 6.5 %multiply_reduce_fusion.2 = f32[256,512]{1,0:T(8,128)S(1)} fusion(f32[16,512]{1,0:T(8,128)S(1)} %neg.6, f32[16,512]{1,0:T(8,128)S(1)} %get-tuple-element.6, f32[16,512,256]{2,1,0:T(8,128)S(1)} %bitcast.122), kind=kOutput, calls=%fused_computation.3 | convolution fusion | flops 6450774016 | bytes 8978432 | tf_op jit(solution)/shard_map/dot_general | solution.py:98
  72.1 3.8 %collective-permute-start.9 = (bf16[256,512]{1,0:T(8,128)(2,1)S(1)}, bf16[256,512]{1,0:T(8,128)(2,1)S(1)}, u32[]{:S(2)}, u32[]{:S(2)}) collective-permute-start(bf16[256,512]{1,0:T(8,128)(2,1)S(1)} %fusion.26), channel_id=1, source_target_pairs={{0,8},{1,9},{2,10},{3,11},{4,12},{5,13},{6,14},{7,15},{8,0},{9,1},... | collective-permute-start | bytes 786440 | tf_op jit(solution)/shard_map/ppermute | solution.py:20
  76.2 12.0 %collective-permute-done.9 = bf16[256,512]{1,0:T(8,128)(2,1)S(1)} collective-permute-done((bf16[256,512]{1,0:T(8,128)(2,1)S(1)}, bf16[256,512]{1,0:T(8,128)(2,1)S(1)}, u32[]{:S(2)}, u32[]{:S(2)}) %collective-permute-start.9) | collective-permute-done | bytes 262176 | tf_op jit(solution)/shard_map/ppermute | solution.py:20
  88.3 4.2 %collective-permute-start.13 = (bf16[2,256,512]{2,1,0:T(8,128)(2,1)S(1)}, bf16[2,256,512]{2,1,0:T(8,128)(2,1)S(1)}, u32[]{:S(2)}, u32[]{:S(2)}) collective-permute-start(bf16[2,256,512]{2,1,0:T(8,128)(2,1)S(1)} %maximum_select_fusion), channel_id=1, source_target_pairs={{0,1},{1,2},{2,3},{3,4},{4,5},{5,6},{6,7},{7,0},{8,9},{9,10},{10,1... | collective-permute-start | bytes 1572872 | tf_op jit(solution)/shard_map/ppermute | solution.py:20
  94.4 6.1 %collective-permute-done.13 = bf16[2,256,512]{2,1,0:T(8,128)(2,1)S(1)} collective-permute-done((bf16[2,256,512]{2,1,0:T(8,128)(2,1)S(1)}, bf16[2,256,512]{2,1,0:T(8,128)(2,1)S(1)}, u32[]{:S(2)}, u32[]{:S(2)}) %collective-permute-start.13) | collective-permute-done | bytes 524320 | tf_op jit(solution)/shard_map/ppermute | solution.py:20
  100.6 5.6 %collective-permute-start.14 = (bf16[2,256,512]{2,1,0:T(8,128)(2,1)S(1)}, bf16[2,256,512]{2,1,0:T(8,128)(2,1)S(1)}, u32[]{:S(2)}, u32[]{:S(2)}) collective-permute-start(bf16[2,256,512]{2,1,0:T(8,128)(2,1)S(1)} %collective-permute-done.13), channel_id=1, source_target_pairs={{0,1},{1,2},{2,3},{3,4},{4,5},{5,6},{6,7},{7,0},{8,9},{9,10},{10,1... | collective-permute-start | bytes 1572872 | tf_op jit(solution)/shard_map/ppermute | solution.py:20
  106.2 1.9 %collective-permute-start.11 = (bf16[2,256,512]{2,1,0:T(8,128)(2,1)S(1)}, bf16[2,256,512]{2,1,0:T(8,128)(2,1)}, u32[]{:S(2)}, u32[]{:S(2)}) collective-permute-start(bf16[2,256,512]{2,1,0:T(8,128)(2,1)S(1)} %collective-permute-done.10), channel_id=1, source_target_pairs={{0,7},{1,0},{2,1},{3,2},{4,3},{5,4},{6,5},{7,6},{8,15},{9,8},{10,9... | collective-permute-start | bytes 1572872 | tf_op jit(solution)/shard_map/ppermute | solution.py:20
  108.1 5.3 %collective-permute-done.14 = bf16[2,256,512]{2,1,0:T(8,128)(2,1)S(1)} collective-permute-done((bf16[2,256,512]{2,1,0:T(8,128)(2,1)S(1)}, bf16[2,256,512]{2,1,0:T(8,128)(2,1)S(1)}, u32[]{:S(2)}, u32[]{:S(2)}) %collective-permute-start.14) | collective-permute-done | bytes 524320 | tf_op jit(solution)/shard_map/ppermute | solution.py:20
  113.4 5.6 %collective-permute-start.15 = (bf16[2,256,512]{2,1,0:T(8,128)(2,1)S(1)}, bf16[2,256,512]{2,1,0:T(8,128)(2,1)S(1)}, u32[]{:S(2)}, u32[]{:S(2)}) collective-permute-start(bf16[2,256,512]{2,1,0:T(8,128)(2,1)S(1)} %collective-permute-done.14), channel_id=1, source_target_pairs={{0,1},{1,2},{2,3},{3,4},{4,5},{5,6},{6,7},{7,0},{8,9},{9,10},{10,1... | collective-permute-start | bytes 1572872 | tf_op jit(solution)/shard_map/ppermute | solution.py:20
  119.1 1.9 %collective-permute-start.12 = (bf16[2,256,512]{2,1,0:T(8,128)(2,1)}, bf16[2,256,512]{2,1,0:T(8,128)(2,1)}, u32[]{:S(2)}, u32[]{:S(2)}) collective-permute-start(bf16[2,256,512]{2,1,0:T(8,128)(2,1)} %collective-permute-done.11), channel_id=1, source_target_pairs={{0,7},{1,0},{2,1},{3,2},{4,3},{5,4},{6,5},{7,6},{8,15},{9,8},{10,9... | collective-permute-start | bytes 1572872 | tf_op jit(solution)/shard_map/ppermute | solution.py:20
  121.1 5.0 %collective-permute-done.15 = bf16[2,256,512]{2,1,0:T(8,128)(2,1)S(1)} collective-permute-done((bf16[2,256,512]{2,1,0:T(8,128)(2,1)S(1)}, bf16[2,256,512]{2,1,0:T(8,128)(2,1)S(1)}, u32[]{:S(2)}, u32[]{:S(2)}) %collective-permute-start.15) | collective-permute-done | bytes 524320 | tf_op jit(solution)/shard_map/ppermute | solution.py:20
  126.1 5.6 %collective-permute-start.16 = (bf16[2,256,512]{2,1,0:T(8,128)(2,1)S(1)}, bf16[2,256,512]{2,1,0:T(8,128)(2,1)S(1)}, u32[]{:S(2)}, u32[]{:S(2)}) collective-permute-start(bf16[2,256,512]{2,1,0:T(8,128)(2,1)S(1)} %collective-permute-done.15), channel_id=1, source_target_pairs={{0,1},{1,2},{2,3},{3,4},{4,5},{5,6},{6,7},{7,0},{8,9},{9,10},{10,1... | collective-permute-start | bytes 1572872 | tf_op jit(solution)/shard_map/ppermute | solution.py:20
  133.5 2.1 %convolution_bitcast_fusion.2 = f32[256,512]{1,0:T(8,128)S(1)} fusion(bf16[2,256,512]{2,1,0:T(8,128)(2,1)S(1)} %collective-permute-done.15, bf16[2,8,512,512]{3,2,1,0:T(8,128)(2,1)} %bitcast.115, s32[]{:T(128)S(6)} %select_n.91), kind=kOutput, calls=%fused_computation.11 | convolution fusion | flops 268435456 | bytes 2097156 | tf_op jit(solution)/shard_map/htc,hco->to/dot_general | solution.py:120
  (51 shorter events, 28.3 us)
Async XLA Ops:
  6.5 32.7 %copy-start.1 = (f32[16,512]{1,0:T(8,128)S(1)}, f32[16,512]{1,0:T(8,128)}, u32[]{:S(2)}) copy-start(f32[16,512]{1,0:T(8,128)} %param.8) | copy-start | bytes 98308
  6.5 125.2 %all-gather.2.cloned.1.call-start = ((), (), s32[]{:S(2)}) async-start(), calls=%async_computation | async-start | bytes 8650752 | tf_op jit(solution)/shard_map/all_gather | solution.py:112
  8.0 11.7 %collective-permute-start = (bf16[3,2,512]{2,1,0:T(2,128)(2,1)S(1)}, bf16[3,2,512]{2,1,0:T(2,128)(2,1)S(1)}, u32[]{:S(2)}, u32[]{:S(2)}) collective-permute-start(bf16[3,2,512]{2,1,0:T(2,128)(2,1)S(1)} %slice.31), channel_id=1, source_target_pairs={{0,16},{16,32},{32,48},{48,64},{64,80},{80,96},{96,112},{112,128},... | collective-permute-start | bytes 18440 | tf_op jit(solution)/shard_map/ppermute | solution.py:16
  21.5 42.2 %copy-start.2 = (f32[16,512]{1,0:T(8,128)S(1)}, f32[16,512]{1,0:T(8,128)}, u32[]{:S(2)}) copy-start(f32[16,512]{1,0:T(8,128)} %param.9) | copy-start | bytes 98308
  23.1 12.0 %collective-permute-start.1 = (f32[16,512]{1,0:T(8,128)S(1)}, f32[16,512]{1,0:T(8,128)S(1)}, u32[]{:S(2)}, u32[]{:S(2)}) collective-permute-start(f32[16,512]{1,0:T(8,128)S(1)} %multiply_reduce_fusion.1), channel_id=1, source_target_pairs={{0,16},{16,32},{32,48},{48,64},{64,80},{80,96},{96,112},{112,128},... | collective-permute-start | bytes 98312 | tf_op jit(solution)/shard_map/ppermute | solution.py:16
  25.0 10.1 %collective-permute-start.2 = (f32[16,512]{1,0:T(8,128)S(1)}, f32[16,512]{1,0:T(8,128)S(1)}, u32[]{:S(2)}, u32[]{:S(2)}) collective-permute-start(f32[16,512]{1,0:T(8,128)S(1)} %multiply_reduce_fusion.1), channel_id=1, source_target_pairs={{0,32},{16,48},{32,64},{48,80},{64,96},{80,112},{96,128},{112,144}... | collective-permute-start | bytes 98312 | tf_op jit(solution)/shard_map/ppermute | solution.py:16
  27.0 9.4 %collective-permute-start.3 = (f32[16,512]{1,0:T(8,128)S(1)}, f32[16,512]{1,0:T(8,128)S(1)}, u32[]{:S(2)}, u32[]{:S(2)}) collective-permute-start(f32[16,512]{1,0:T(8,128)S(1)} %multiply_reduce_fusion.1), channel_id=1, source_target_pairs={{0,48},{16,64},{32,80},{48,96},{64,112},{80,128},{96,144},{112,160... | collective-permute-start | bytes 98312 | tf_op jit(solution)/shard_map/ppermute | solution.py:16
  28.9 10.3 %collective-permute-start.4 = (f32[16,512]{1,0:T(8,128)S(1)}, f32[16,512]{1,0:T(8,128)S(1)}, u32[]{:S(2)}, u32[]{:S(2)}) collective-permute-start(f32[16,512]{1,0:T(8,128)S(1)} %multiply_reduce_fusion.1), channel_id=1, source_target_pairs={{0,64},{16,80},{32,96},{48,112},{64,128},{80,144},{96,160},{112,17... | collective-permute-start | bytes 98312 | tf_op jit(solution)/shard_map/ppermute | solution.py:16
  39.3 10.9 %collective-permute-start.5 = (f32[16,512]{1,0:T(8,128)S(1)}, f32[16,512]{1,0:T(8,128)S(1)}, u32[]{:S(2)}, u32[]{:S(2)}) collective-permute-start(f32[16,512]{1,0:T(8,128)S(1)} %multiply_add_fusion.1), channel_id=1, source_target_pairs={{0,64},{16,80},{32,96},{48,112},{64,128},{80,144},{96,160},{112,17... | collective-permute-start | bytes 98312 | tf_op jit(solution)/shard_map/ppermute | solution.py:16
  42.5 11.4 %collective-permute-start.6 = (f32[16,512]{1,0:T(8,128)S(1)}, f32[16,512]{1,0:T(8,128)S(1)}, u32[]{:S(2)}, u32[]{:S(2)}) collective-permute-start(f32[16,512]{1,0:T(8,128)S(1)} %multiply_add_fusion.1), channel_id=1, source_target_pairs={{0,128},{16,144},{32,160},{48,176},{64,192},{80,208},{96,224},{112... | collective-permute-start | bytes 98312 | tf_op jit(solution)/shard_map/ppermute | solution.py:16
  48.3 9.0 %collective-permute-start.7 = (f32[16,512]{1,0:T(8,128)S(1)}, f32[16,512]{1,0:T(8,128)S(1)}, u32[]{:S(2)}, u32[]{:S(2)}) collective-permute-start(f32[16,512]{1,0:T(8,128)S(1)} %multiply_add_fusion.1), channel_id=1, source_target_pairs={{0,192},{16,208},{32,224},{48,240},{64,256},{80,272},{96,288},{112... | collective-permute-start | bytes 98312 | tf_op jit(solution)/shard_map/ppermute | solution.py:16
  57.3 6.4 %collective-permute-start.8 = (f32[16,512]{1,0:T(8,128)S(1)}, f32[16,512]{1,0:T(8,128)S(1)}, u32[]{:S(2)}, u32[]{:S(2)}) collective-permute-start(f32[16,512]{1,0:T(8,128)S(1)} %multiply_add_fusion), channel_id=1, source_target_pairs={{0,256},{16,272},{32,288},{48,304},{64,320},{80,336},{96,352},{112... | collective-permute-start | bytes 98312 | tf_op jit(solution)/shard_map/ppermute | solution.py:16
  60.2 11.6 %copy-start.3 = (f32[512]{0:T(512)S(1)}, f32[512]{0:T(512)}, u32[]{:S(2)}) copy-start(f32[512]{0:T(512)} %param.10) | copy-start | bytes 6148
  72.1 16.1 %collective-permute-start.9 = (bf16[256,512]{1,0:T(8,128)(2,1)S(1)}, bf16[256,512]{1,0:T(8,128)(2,1)S(1)}, u32[]{:S(2)}, u32[]{:S(2)}) collective-permute-start(bf16[256,512]{1,0:T(8,128)(2,1)S(1)} %fusion.26), channel_id=1, source_target_pairs={{0,8},{1,9},{2,10},{3,11},{4,12},{5,13},{6,14},{7,15},{8,0},{9,1},... | collective-permute-start | bytes 786440 | tf_op jit(solution)/shard_map/ppermute | solution.py:20
  88.3 12.2 %collective-permute-start.13 = (bf16[2,256,512]{2,1,0:T(8,128)(2,1)S(1)}, bf16[2,256,512]{2,1,0:T(8,128)(2,1)S(1)}, u32[]{:S(2)}, u32[]{:S(2)}) collective-permute-start(bf16[2,256,512]{2,1,0:T(8,128)(2,1)S(1)} %maximum_select_fusion), channel_id=1, source_target_pairs={{0,1},{1,2},{2,3},{3,4},{4,5},{5,6},{6,7},{7,0},{8,9},{9,10},{10,1... | collective-permute-start | bytes 1572872 | tf_op jit(solution)/shard_map/ppermute | solution.py:20
  92.5 13.7 %collective-permute-start.10 = (bf16[2,256,512]{2,1,0:T(8,128)(2,1)S(1)}, bf16[2,256,512]{2,1,0:T(8,128)(2,1)S(1)}, u32[]{:S(2)}, u32[]{:S(2)}) collective-permute-start(bf16[2,256,512]{2,1,0:T(8,128)(2,1)S(1)} %maximum_select_fusion), channel_id=1, source_target_pairs={{0,7},{1,0},{2,1},{3,2},{4,3},{5,4},{6,5},{7,6},{8,15},{9,8},{10,9... | collective-permute-start | bytes 1572872 | tf_op jit(solution)/shard_map/ppermute | solution.py:20
  100.6 12.8 %collective-permute-start.14 = (bf16[2,256,512]{2,1,0:T(8,128)(2,1)S(1)}, bf16[2,256,512]{2,1,0:T(8,128)(2,1)S(1)}, u32[]{:S(2)}, u32[]{:S(2)}) collective-permute-start(bf16[2,256,512]{2,1,0:T(8,128)(2,1)S(1)} %collective-permute-done.13), channel_id=1, source_target_pairs={{0,1},{1,2},{2,3},{3,4},{4,5},{5,6},{6,7},{7,0},{8,9},{9,10},{10,1... | collective-permute-start | bytes 1572872 | tf_op jit(solution)/shard_map/ppermute | solution.py:20
  106.2 13.0 %collective-permute-start.11 = (bf16[2,256,512]{2,1,0:T(8,128)(2,1)S(1)}, bf16[2,256,512]{2,1,0:T(8,128)(2,1)}, u32[]{:S(2)}, u32[]{:S(2)}) collective-permute-start(bf16[2,256,512]{2,1,0:T(8,128)(2,1)S(1)} %collective-permute-done.10), channel_id=1, source_target_pairs={{0,7},{1,0},{2,1},{3,2},{4,3},{5,4},{6,5},{7,6},{8,15},{9,8},{10,9... | collective-permute-start | bytes 1572872 | tf_op jit(solution)/shard_map/ppermute | solution.py:20
  113.4 12.7 %collective-permute-start.15 = (bf16[2,256,512]{2,1,0:T(8,128)(2,1)S(1)}, bf16[2,256,512]{2,1,0:T(8,128)(2,1)S(1)}, u32[]{:S(2)}, u32[]{:S(2)}) collective-permute-start(bf16[2,256,512]{2,1,0:T(8,128)(2,1)S(1)} %collective-permute-done.14), channel_id=1, source_target_pairs={{0,1},{1,2},{2,3},{3,4},{4,5},{5,6},{6,7},{7,0},{8,9},{9,10},{10,1... | collective-permute-start | bytes 1572872 | tf_op jit(solution)/shard_map/ppermute | solution.py:20
  119.1 21.8 %collective-permute-start.12 = (bf16[2,256,512]{2,1,0:T(8,128)(2,1)}, bf16[2,256,512]{2,1,0:T(8,128)(2,1)}, u32[]{:S(2)}, u32[]{:S(2)}) collective-permute-start(bf16[2,256,512]{2,1,0:T(8,128)(2,1)} %collective-permute-done.11), channel_id=1, source_target_pairs={{0,7},{1,0},{2,1},{3,2},{4,3},{5,4},{6,5},{7,6},{8,15},{9,8},{10,9... | collective-permute-start | bytes 1572872 | tf_op jit(solution)/shard_map/ppermute | solution.py:20
  126.1 16.3 %collective-permute-start.16 = (bf16[2,256,512]{2,1,0:T(8,128)(2,1)S(1)}, bf16[2,256,512]{2,1,0:T(8,128)(2,1)S(1)}, u32[]{:S(2)}, u32[]{:S(2)}) collective-permute-start(bf16[2,256,512]{2,1,0:T(8,128)(2,1)S(1)} %collective-permute-done.15), channel_id=1, source_target_pairs={{0,1},{1,2},{2,3},{3,4},{4,5},{5,6},{6,7},{7,0},{8,9},{9,10},{10,1... | collective-permute-start | bytes 1572872 | tf_op jit(solution)/shard_map/ppermute | solution.py:20
  131.7 7.2 %copy-start = (bf16[8192,512]{1,0:T(8,128)(2,1)S(1)}, bf16[8192,512]{1,0:T(8,128)(2,1)}, u32[]{:S(2)}) copy-start(bf16[8192,512]{1,0:T(8,128)(2,1)} %all-gather.2.cloned.1.call-done) | copy-start | bytes 25165828
Sparse Core Ops, SparseCore 0:
  9.5 83.6 all-gather.1

commit v2 on v1

--- a/solution.py
+++ b/solution.py
@@ -46,21 +46,14 @@
 
 def entering_state(local_state, rate, tokens_here, axis):
     sections = lax.axis_size(axis)
-    state = jnp.zeros_like(local_state)
-    for distance in range(1, min(4, sections - 1) + 1):
-        lag = distance - 1
-        state = state + jnp.exp(-rate * (tokens_here * lag)) * passed_along(local_state, axis, distance)
-    width = 4
-    while width < sections:
-        grown = state
-        for step in range(1, 4):
-            distance = width * step
-            if distance >= sections:
-                break
-            grown = grown + jnp.exp(-rate * (tokens_here * distance)) * passed_along(state, axis, distance)
-        state = grown
-        width *= 4
-    return state
+    spread = jnp.broadcast_to(local_state[None], (sections,) + local_state.shape)
+    states = lax.all_to_all(spread, axis, 0, 0)
+    here = lax.axis_index(axis)
+    earlier = jnp.arange(sections)
+    lag = jnp.maximum(here - 1 - earlier, 0).astype(jnp.float32)[:, None, None]
+    weight = jnp.exp(-rate[None] * (tokens_here * lag))
+    taken = (earlier < here)[:, None, None]
+    return jnp.sum(jnp.where(taken, weight * states, 0.0), axis=0)
 
 
 def body(qkv, conv_weight, decay_rate, residue, skip_gain, out_weight):

time: 151 us -> 170 us (1.13)
  the two profiles are of different devices: /device:TPU:26 before, /device:TPU:30 now
where the time goes in v2:
time: 170 us
  waiting for transfers between devices  75.3 us (44%)
  starting transfers between devices  39.2 us (23%)
  matrix products  25.8 us (15%)
  between operations  13.9 us (8%)
  other arithmetic  11.6 us (7%)
  local copies, waits for them, and re-layouts  3.78 us (2%)
    ppermute x8, waiting for transfers between devices, shifted(): return lax.ppermute(block, axis, route)  34.5 us
    all_to_all x1, waiting for transfers between devices, entering_state(): states = lax.all_to_all(spread, axis, 0, 0)  31.6 us
    ppermute x8, starting transfers between devices, shifted(): return lax.ppermute(block, axis, route)  31.2 us
    dot_general x1, matrix products, finish(): jnp.dot(lower, scaled, precision=PRECISE)  14 us
    dot_general x8, matrix products, tail(): jnp.einsum('htc,hco->to', features[r], taken, preferred_element_type=jnp....  11.8 us
    ppermute x1, waiting for transfers between devices, passed_along(): return lax.ppermute(block, axis, route)  8.35 us
    all_to_all x1, starting transfers between devices, entering_state(): states = lax.all_to_all(spread, axis, 0, 0)  6.11 us
    mul x1, other arithmetic, finish(): growth * product[:, None, :]  4.94 us
  transfers between devices with their start and end apart: 11, of which 6 were waited for; matrix products, arithmetic and copies ran while one was open for 24% of the time, Pallas kernels for 0%

profile of v2, /device:TPU:30, one launch (start us, length us, event | category | flops | bytes accessed | tf_op | source)
XLA Modules:
  0.0 169.5 jit_solution(181250574054178131)
XLA Ops:
  8.0 1.9 %collective-permute-start = (bf16[3,2,512]{2,1,0:T(2,128)(2,1)S(1)}, bf16[3,2,512]{2,1,0:T(2,128)(2,1)S(1)}, u32[]{:S(2)}, u32[]{:S(2)}) collective-permute-start(bf16[3,2,512]{2,1,0:T(2,128)(2,1)S(1)} %slice.31), channel_id=1, source_target_pairs={{0,16},{16,32},{32,48},{48,64},{64,80},{80,96},{96,112},{112,128},... | collective-permute-start | bytes 18440 | tf_op jit(solution)/shard_map/ppermute | solution.py:16
  11.6 8.4 %collective-permute-done = bf16[3,2,512]{2,1,0:T(2,128)(2,1)S(1)} collective-permute-done((bf16[3,2,512]{2,1,0:T(2,128)(2,1)S(1)}, bf16[3,2,512]{2,1,0:T(2,128)(2,1)S(1)}, u32[]{:S(2)}, u32[]{:S(2)}) %collective-permute-start) | collective-permute-done | bytes 6176 | tf_op jit(solution)/shard_map/ppermute | solution.py:16
  24.5 6.1 %all-to-all-start = ((f32[32,16,512]{2,1,0:T(8,128)}), f32[32,16,512]{2,1,0:T(8,128)S(1)}, u32[]{:S(2)}, u32[]{:S(2)}) async-start(f32[32,16,512]{2,1,0:T(8,128)} %broadcast_in_dim.11), calls=%async_computation | async-start | bytes 2097152 | tf_op jit(solution)/shard_map/all_to_all | solution.py:50
  31.7 4.9 %bitcast_multiply_fusion = f32[256,8192]{0,1:T(8,128)} fusion(f32[256,512]{0,1:T(8,128)} %copy.45, f32[8192]{0:T(1024)S(1)} %bitcast.125), kind=kLoop, calls=%fused_computation | loop fusion | flops 4194304 | bytes 8945664 | tf_op jit(solution)/shard_map/mul | solution.py:89
  36.7 31.6 %all-to-all-done = f32[32,16,512]{2,1,0:T(8,128)S(1)} async-done(((f32[32,16,512]{2,1,0:T(8,128)}), f32[32,16,512]{2,1,0:T(8,128)S(1)}, u32[]{:S(2)}, u32[]{:S(2)}) %all-to-all-start) | async-done | bytes 1048608 | tf_op jit(solution)/shard_map/all_to_all | solution.py:50
  70.1 14.0 %multiply_reduce_fusion.2 = f32[256,512]{1,0:T(8,128)S(1)} fusion(f32[16,512]{1,0:T(8,128)S(1)} %neg.11, f32[16,512]{1,0:T(8,128)S(1)} %get-tuple-element.6, f32[16,512,256]{2,1,0:T(8,128)} %bitcast.122), kind=kOutput, calls=%fused_computation.3 | convolution fusion | flops 6450774016 | bytes 8978432 | tf_op jit(solution)/shard_map/dot_general | solution.py:91
  84.4 3.7 %collective-permute-start.1 = (bf16[256,512]{1,0:T(8,128)(2,1)S(1)}, bf16[256,512]{1,0:T(8,128)(2,1)S(1)}, u32[]{:S(2)}, u32[]{:S(2)}) collective-permute-start(bf16[256,512]{1,0:T(8,128)(2,1)S(1)} %fusion.26), channel_id=1, source_target_pairs={{0,8},{1,9},{2,10},{3,11},{4,12},{5,13},{6,14},{7,15},{8,0},{9,1},... | collective-permute-start | bytes 786440 | tf_op jit(solution)/shard_map/ppermute | solution.py:20
  88.5 13.4 %collective-permute-done.1 = bf16[256,512]{1,0:T(8,128)(2,1)S(1)} collective-permute-done((bf16[256,512]{1,0:T(8,128)(2,1)S(1)}, bf16[256,512]{1,0:T(8,128)(2,1)S(1)}, u32[]{:S(2)}, u32[]{:S(2)}) %collective-permute-start.1) | collective-permute-done | bytes 262176 | tf_op jit(solution)/shard_map/ppermute | solution.py:20
  101.9 4.9 %collective-permute-start.5 = (bf16[2,256,512]{2,1,0:T(8,128)(2,1)S(1)}, bf16[2,256,512]{2,1,0:T(8,128)(2,1)S(1)}, u32[]{:S(2)}, u32[]{:S(2)}) collective-permute-start(bf16[2,256,512]{2,1,0:T(8,128)(2,1)S(1)} %maximum_select_fusion), channel_id=1, source_target_pairs={{0,1},{1,2},{2,3},{3,4},{4,5},{5,6},{6,7},{7,0},{8,9},{9,10},{10,1... | collective-permute-start | bytes 1572872 | tf_op jit(solution)/shard_map/ppermute | solution.py:20
  106.9 1.9 %collective-permute-start.2 = (bf16[2,256,512]{2,1,0:T(8,128)(2,1)S(1)}, bf16[2,256,512]{2,1,0:T(8,128)(2,1)S(1)}, u32[]{:S(2)}, u32[]{:S(2)}) collective-permute-start(bf16[2,256,512]{2,1,0:T(8,128)(2,1)S(1)} %maximum_select_fusion), channel_id=1, source_target_pairs={{0,7},{1,0},{2,1},{3,2},{4,3},{5,4},{6,5},{7,6},{8,15},{9,8},{10,9... | collective-permute-start | bytes 1572872 | tf_op jit(solution)/shard_map/ppermute | solution.py:20
  108.8 8.0 %collective-permute-done.5 = bf16[2,256,512]{2,1,0:T(8,128)(2,1)S(1)} collective-permute-done((bf16[2,256,512]{2,1,0:T(8,128)(2,1)S(1)}, bf16[2,256,512]{2,1,0:T(8,128)(2,1)S(1)}, u32[]{:S(2)}, u32[]{:S(2)}) %collective-permute-start.5) | collective-permute-done | bytes 524320 | tf_op jit(solution)/shard_map/ppermute | solution.py:20
  116.8 5.6 %collective-permute-start.6 = (bf16[2,256,512]{2,1,0:T(8,128)(2,1)S(1)}, bf16[2,256,512]{2,1,0:T(8,128)(2,1)S(1)}, u32[]{:S(2)}, u32[]{:S(2)}) collective-permute-start(bf16[2,256,512]{2,1,0:T(8,128)(2,1)S(1)} %collective-permute-done.5), channel_id=1, source_target_pairs={{0,1},{1,2},{2,3},{3,4},{4,5},{5,6},{6,7},{7,0},{8,9},{9,10},{10,1... | collective-permute-start | bytes 1572872 | tf_op jit(solution)/shard_map/ppermute | solution.py:20
  122.4 1.9 %collective-permute-start.3 = (bf16[2,256,512]{2,1,0:T(8,128)(2,1)S(1)}, bf16[2,256,512]{2,1,0:T(8,128)(2,1)}, u32[]{:S(2)}, u32[]{:S(2)}) collective-permute-start(bf16[2,256,512]{2,1,0:T(8,128)(2,1)S(1)} %collective-permute-done.2), channel_id=1, source_target_pairs={{0,7},{1,0},{2,1},{3,2},{4,3},{5,4},{6,5},{7,6},{8,15},{9,8},{10,9... | collective-permute-start | bytes 1572872 | tf_op jit(solution)/shard_map/ppermute | solution.py:20
  124.3 7.1 %collective-permute-done.6 = bf16[2,256,512]{2,1,0:T(8,128)(2,1)S(1)} collective-permute-done((bf16[2,256,512]{2,1,0:T(8,128)(2,1)S(1)}, bf16[2,256,512]{2,1,0:T(8,128)(2,1)S(1)}, u32[]{:S(2)}, u32[]{:S(2)}) %collective-permute-start.6) | collective-permute-done | bytes 524320 | tf_op jit(solution)/shard_map/ppermute | solution.py:20
  131.4 5.6 %collective-permute-start.7 = (bf16[2,256,512]{2,1,0:T(8,128)(2,1)S(1)}, bf16[2,256,512]{2,1,0:T(8,128)(2,1)S(1)}, u32[]{:S(2)}, u32[]{:S(2)}) collective-permute-start(bf16[2,256,512]{2,1,0:T(8,128)(2,1)S(1)} %collective-permute-done.6), channel_id=1, source_target_pairs={{0,1},{1,2},{2,3},{3,4},{4,5},{5,6},{6,7},{7,0},{8,9},{9,10},{10,1... | collective-permute-start | bytes 1572872 | tf_op jit(solution)/shard_map/ppermute | solution.py:20
  137.2 1.9 %collective-permute-start.4 = (bf16[2,256,512]{2,1,0:T(8,128)(2,1)}, bf16[2,256,512]{2,1,0:T(8,128)(2,1)}, u32[]{:S(2)}, u32[]{:S(2)}) collective-permute-start(bf16[2,256,512]{2,1,0:T(8,128)(2,1)} %collective-permute-done.3), channel_id=1, source_target_pairs={{0,7},{1,0},{2,1},{3,2},{4,3},{5,4},{6,5},{7,6},{8,15},{9,8},{10,9... | collective-permute-start | bytes 1572872 | tf_op jit(solution)/shard_map/ppermute | solution.py:20
  139.1 6.1 %collective-permute-done.7 = bf16[2,256,512]{2,1,0:T(8,128)(2,1)S(1)} collective-permute-done((bf16[2,256,512]{2,1,0:T(8,128)(2,1)S(1)}, bf16[2,256,512]{2,1,0:T(8,128)(2,1)S(1)}, u32[]{:S(2)}, u32[]{:S(2)}) %collective-permute-start.7) | collective-permute-done | bytes 524320 | tf_op jit(solution)/shard_map/ppermute | solution.py:20
  145.2 5.6 %collective-permute-start.8 = (bf16[2,256,512]{2,1,0:T(8,128)(2,1)S(1)}, bf16[2,256,512]{2,1,0:T(8,128)(2,1)S(1)}, u32[]{:S(2)}, u32[]{:S(2)}) collective-permute-start(bf16[2,256,512]{2,1,0:T(8,128)(2,1)S(1)} %collective-permute-done.7), channel_id=1, source_target_pairs={{0,1},{1,2},{2,3},{3,4},{4,5},{5,6},{6,7},{7,0},{8,9},{9,10},{10,1... | collective-permute-start | bytes 1572872 | tf_op jit(solution)/shard_map/ppermute | solution.py:20
  150.8 1.8 %convolution_bitcast_fusion.6 = f32[256,512]{1,0:T(8,128)S(1)} fusion(bf16[2,256,512]{2,1,0:T(8,128)(2,1)S(1)} %collective-permute-done.2, bf16[2,8,512,512]{3,2,1,0:T(8,128)(2,1)} %bitcast.114, s32[]{:T(128)S(6)} %select_n.88), kind=kOutput, calls=%fused_computation.15 | convolution fusion | flops 268435456 | bytes 2097156 | tf_op jit(solution)/shard_map/htc,hco->to/dot_general | solution.py:113
  152.6 2.1 %convolution_bitcast_fusion.2 = f32[256,512]{1,0:T(8,128)S(1)} fusion(bf16[2,256,512]{2,1,0:T(8,128)(2,1)S(1)} %collective-permute-done.7, bf16[2,8,512,512]{3,2,1,0:T(8,128)(2,1)} %bitcast.115, s32[]{:T(128)S(6)} %select_n.96), kind=kOutput, calls=%fused_computation.11 | convolution fusion | flops 268435456 | bytes 2097156 | tf_op jit(solution)/shard_map/htc,hco->to/dot_general | solution.py:113
  154.7 1.7 convolution_bitcast_fusion.1
  156.4 1.7 convolution_bitcast_fusion
  158.5 1.5 fusion.3
  160.0 1.5 fusion.4
  (39 shorter events, 12.8 us)
Async XLA Ops:
  6.5 144.3 %all-gather.2.cloned.1.call-start = ((), (), s32[]{:S(2)}) async-start(), calls=%async_computation.1 | async-start | bytes 8650752 | tf_op jit(solution)/shard_map/all_gather | solution.py:105
  8.0 12.0 %collective-permute-start = (bf16[3,2,512]{2,1,0:T(2,128)(2,1)S(1)}, bf16[3,2,512]{2,1,0:T(2,128)(2,1)S(1)}, u32[]{:S(2)}, u32[]{:S(2)}) collective-permute-start(bf16[3,2,512]{2,1,0:T(2,128)(2,1)S(1)} %slice.31), channel_id=1, source_target_pairs={{0,16},{16,32},{32,48},{48,64},{64,80},{80,96},{96,112},{112,128},... | collective-permute-start | bytes 18440 | tf_op jit(solution)/shard_map/ppermute | solution.py:16
  11.6 19.0 %copy-start.1 = (f32[16,512]{1,0:T(8,128)S(1)}, f32[16,512]{1,0:T(8,128)}, u32[]{:S(2)}) copy-start(f32[16,512]{1,0:T(8,128)} %param.8) | copy-start | bytes 98308
  21.9 46.7 %copy-start.2 = (f32[16,512]{1,0:T(8,128)S(1)}, f32[16,512]{1,0:T(8,128)}, u32[]{:S(2)}) copy-start(f32[16,512]{1,0:T(8,128)} %param.9) | copy-start | bytes 98308
  24.5 43.8 %all-to-all-start = ((f32[32,16,512]{2,1,0:T(8,128)}), f32[32,16,512]{2,1,0:T(8,128)S(1)}, u32[]{:S(2)}, u32[]{:S(2)}) async-start(f32[32,16,512]{2,1,0:T(8,128)} %broadcast_in_dim.11), calls=%async_computation | async-start | bytes 2097152 | tf_op jit(solution)/shard_map/all_to_all | solution.py:50
  36.7 47.4 %copy-start.3 = (f32[512]{0:T(512)S(1)}, f32[512]{0:T(512)}, u32[]{:S(2)}) copy-start(f32[512]{0:T(512)} %param.10) | copy-start | bytes 6148
  84.4 17.4 %collective-permute-start.1 = (bf16[256,512]{1,0:T(8,128)(2,1)S(1)}, bf16[256,512]{1,0:T(8,128)(2,1)S(1)}, u32[]{:S(2)}, u32[]{:S(2)}) collective-permute-start(bf16[256,512]{1,0:T(8,128)(2,1)S(1)} %fusion.26), channel_id=1, source_target_pairs={{0,8},{1,9},{2,10},{3,11},{4,12},{5,13},{6,14},{7,15},{8,0},{9,1},... | collective-permute-start | bytes 786440 | tf_op jit(solution)/shard_map/ppermute | solution.py:20
  101.9 14.8 %collective-permute-start.5 = (bf16[2,256,512]{2,1,0:T(8,128)(2,1)S(1)}, bf16[2,256,512]{2,1,0:T(8,128)(2,1)S(1)}, u32[]{:S(2)}, u32[]{:S(2)}) collective-permute-start(bf16[2,256,512]{2,1,0:T(8,128)(2,1)S(1)} %maximum_select_fusion), channel_id=1, source_target_pairs={{0,1},{1,2},{2,3},{3,4},{4,5},{5,6},{6,7},{7,0},{8,9},{9,10},{10,1... | collective-permute-start | bytes 1572872 | tf_op jit(solution)/shard_map/ppermute | solution.py:20
  106.9 15.5 %collective-permute-start.2 = (bf16[2,256,512]{2,1,0:T(8,128)(2,1)S(1)}, bf16[2,256,512]{2,1,0:T(8,128)(2,1)S(1)}, u32[]{:S(2)}, u32[]{:S(2)}) collective-permute-start(bf16[2,256,512]{2,1,0:T(8,128)(2,1)S(1)} %maximum_select_fusion), channel_id=1, source_target_pairs={{0,7},{1,0},{2,1},{3,2},{4,3},{5,4},{6,5},{7,6},{8,15},{9,8},{10,9... | collective-permute-start | bytes 1572872 | tf_op jit(solution)/shard_map/ppermute | solution.py:20
  116.8 14.6 %collective-permute-start.6 = (bf16[2,256,512]{2,1,0:T(8,128)(2,1)S(1)}, bf16[2,256,512]{2,1,0:T(8,128)(2,1)S(1)}, u32[]{:S(2)}, u32[]{:S(2)}) collective-permute-start(bf16[2,256,512]{2,1,0:T(8,128)(2,1)S(1)} %collective-permute-done.5), channel_id=1, source_target_pairs={{0,1},{1,2},{2,3},{3,4},{4,5},{5,6},{6,7},{7,0},{8,9},{9,10},{10,1... | collective-permute-start | bytes 1572872 | tf_op jit(solution)/shard_map/ppermute | solution.py:20
  122.4 14.8 %collective-permute-start.3 = (bf16[2,256,512]{2,1,0:T(8,128)(2,1)S(1)}, bf16[2,256,512]{2,1,0:T(8,128)(2,1)}, u32[]{:S(2)}, u32[]{:S(2)}) collective-permute-start(bf16[2,256,512]{2,1,0:T(8,128)(2,1)S(1)} %collective-permute-done.2), channel_id=1, source_target_pairs={{0,7},{1,0},{2,1},{3,2},{4,3},{5,4},{6,5},{7,6},{8,15},{9,8},{10,9... | collective-permute-start | bytes 1572872 | tf_op jit(solution)/shard_map/ppermute | solution.py:20
  131.4 13.8 %collective-permute-start.7 = (bf16[2,256,512]{2,1,0:T(8,128)(2,1)S(1)}, bf16[2,256,512]{2,1,0:T(8,128)(2,1)S(1)}, u32[]{:S(2)}, u32[]{:S(2)}) collective-permute-start(bf16[2,256,512]{2,1,0:T(8,128)(2,1)S(1)} %collective-permute-done.6), channel_id=1, source_target_pairs={{0,1},{1,2},{2,3},{3,4},{4,5},{5,6},{6,7},{7,0},{8,9},{9,10},{10,1... | collective-permute-start | bytes 1572872 | tf_op jit(solution)/shard_map/ppermute | solution.py:20
  137.2 22.8 %collective-permute-start.4 = (bf16[2,256,512]{2,1,0:T(8,128)(2,1)}, bf16[2,256,512]{2,1,0:T(8,128)(2,1)}, u32[]{:S(2)}, u32[]{:S(2)}) collective-permute-start(bf16[2,256,512]{2,1,0:T(8,128)(2,1)} %collective-permute-done.3), channel_id=1, source_target_pairs={{0,7},{1,0},{2,1},{3,2},{4,3},{5,4},{6,5},{7,6},{8,15},{9,8},{10,9... | collective-permute-start | bytes 1572872 | tf_op jit(solution)/shard_map/ppermute | solution.py:20
  145.2 16.3 %collective-permute-start.8 = (bf16[2,256,512]{2,1,0:T(8,128)(2,1)S(1)}, bf16[2,256,512]{2,1,0:T(8,128)(2,1)S(1)}, u32[]{:S(2)}, u32[]{:S(2)}) collective-permute-start(bf16[2,256,512]{2,1,0:T(8,128)(2,1)S(1)} %collective-permute-done.7), channel_id=1, source_target_pairs={{0,1},{1,2},{2,3},{3,4},{4,5},{5,6},{6,7},{7,0},{8,9},{9,10},{10,1... | collective-permute-start | bytes 1572872 | tf_op jit(solution)/shard_map/ppermute | solution.py:20
  150.8 7.3 %copy-start = (bf16[8192,512]{1,0:T(8,128)(2,1)S(1)}, bf16[8192,512]{1,0:T(8,128)(2,1)}, u32[]{:S(2)}) copy-start(bf16[8192,512]{1,0:T(8,128)(2,1)} %all-gather.2.cloned.1.call-done) | copy-start | bytes 25165828
Sparse Core Ops, SparseCore 0:
  9.5 100.2 all-gather.1

commit v3 on v1

--- a/solution.py
+++ b/solution.py
@@ -36,11 +36,18 @@
     ahead, behind = [], []
     up, down = chunk, chunk
     for step in range(ring // 2):
-        up = shifted(up, axis, forward)
-        behind.append(up)
         if step < (ring - 1) // 2:
+            up = shifted(up, axis, forward)
+            behind.append(up)
             down = shifted(down, axis, backward)
             ahead.append(down)
+        elif halves == 2:
+            up = shifted(up[:1], axis, forward)
+            down = shifted(down[1:], axis, backward)
+            behind.append(jnp.concatenate([up, down]))
+        else:
+            up = shifted(up, axis, forward)
+            behind.append(up)
     return [chunk] + ahead + behind[::-1]
 
 

time: 151 us -> 155 us (1.026)
  the two profiles are of different devices: /device:TPU:26 before, /device:TPU:4 now
where the time goes in v3:
time: 155 us; the launch traced here: 154 us
  starting transfers between devices  74.7 us (48%)
  waiting for transfers between devices  37.2 us (24%)
  matrix products  18.3 us (12%)
  between operations  14 us (9%)
  other arithmetic  7.66 us (5%)
  local copies, waits for them, and re-layouts  2.6 us (2%)
    ppermute x9, starting transfers between devices, passed_along(): return lax.ppermute(block, axis, route)  44 us
    ppermute x9, waiting for transfers between devices, shifted(): return lax.ppermute(block, axis, route)  32.7 us
    ppermute x9, starting transfers between devices, shifted(): return lax.ppermute(block, axis, route)  30.7 us
    dot_general x8, matrix products, tail(): jnp.einsum('htc,hco->to', features[r], taken, preferred_element_type=jnp....  11.8 us
    dot_general x1, matrix products, finish(): jnp.dot(lower, scaled, precision=PRECISE)  6.54 us
    ppermute x9, waiting for transfers between devices, passed_along(): return lax.ppermute(block, axis, route)  3.73 us
  transfers between devices with their start and end apart: 19, of which 7 were waited for; matrix products, arithmetic and copies ran while one was open for 17% of the time, Pallas kernels for 0%

profile of v3, /device:TPU:4, one launch (start us, length us, event | category | flops | bytes accessed | tf_op | source)
XLA Modules:
  0.0 154.5 jit_solution(358642158611692297)
XLA Ops:
  14.9 4.6 %collective-permute-start.1 = (f32[16,512]{1,0:T(8,128)S(1)}, f32[16,512]{1,0:T(8,128)S(1)}, u32[]{:S(2)}, u32[]{:S(2)}) collective-permute-start(f32[16,512]{1,0:T(8,128)S(1)} %multiply_reduce_fusion.1), channel_id=1, source_target_pairs={{0,16},{16,32},{32,48},{48,64},{64,80},{80,96},{96,112},{112,128},... | collective-permute-start | bytes 98312 | tf_op jit(solution)/shard_map/ppermute | solution.py:16
  19.4 4.3 %collective-permute-start.2 = (f32[16,512]{1,0:T(8,128)S(1)}, f32[16,512]{1,0:T(8,128)S(1)}, u32[]{:S(2)}, u32[]{:S(2)}) collective-permute-start(f32[16,512]{1,0:T(8,128)S(1)} %multiply_reduce_fusion.1), channel_id=1, source_target_pairs={{0,32},{16,48},{32,64},{48,80},{64,96},{80,112},{96,128},{112,144}... | collective-permute-start | bytes 98312 | tf_op jit(solution)/shard_map/ppermute | solution.py:16
  23.7 5.0 %collective-permute-start.3 = (f32[16,512]{1,0:T(8,128)S(1)}, f32[16,512]{1,0:T(8,128)S(1)}, u32[]{:S(2)}, u32[]{:S(2)}) collective-permute-start(f32[16,512]{1,0:T(8,128)S(1)} %multiply_reduce_fusion.1), channel_id=1, source_target_pairs={{0,48},{16,64},{32,80},{48,96},{64,112},{80,128},{96,144},{112,160... | collective-permute-start | bytes 98312 | tf_op jit(solution)/shard_map/ppermute | solution.py:16
  28.7 6.4 %collective-permute-start.4 = (f32[16,512]{1,0:T(8,128)S(1)}, f32[16,512]{1,0:T(8,128)S(1)}, u32[]{:S(2)}, u32[]{:S(2)}) collective-permute-start(f32[16,512]{1,0:T(8,128)S(1)} %multiply_reduce_fusion.1), channel_id=1, source_target_pairs={{0,64},{16,80},{32,96},{48,112},{64,128},{80,144},{96,160},{112,17... | collective-permute-start | bytes 98312 | tf_op jit(solution)/shard_map/ppermute | solution.py:16
  36.9 5.3 %collective-permute-start.5 = (f32[16,512]{1,0:T(8,128)S(1)}, f32[16,512]{1,0:T(8,128)S(1)}, u32[]{:S(2)}, u32[]{:S(2)}) collective-permute-start(f32[16,512]{1,0:T(8,128)S(1)} %multiply_add_fusion.1), channel_id=1, source_target_pairs={{0,64},{16,80},{32,96},{48,112},{64,128},{80,144},{96,160},{112,17... | collective-permute-start | bytes 98312 | tf_op jit(solution)/shard_map/ppermute | solution.py:16
  42.2 5.8 %collective-permute-start.6 = (f32[16,512]{1,0:T(8,128)S(1)}, f32[16,512]{1,0:T(8,128)S(1)}, u32[]{:S(2)}, u32[]{:S(2)}) collective-permute-start(f32[16,512]{1,0:T(8,128)S(1)} %multiply_add_fusion.1), channel_id=1, source_target_pairs={{0,128},{16,144},{32,160},{48,176},{64,192},{80,208},{96,224},{112... | collective-permute-start | bytes 98312 | tf_op jit(solution)/shard_map/ppermute | solution.py:16
  48.0 7.0 %collective-permute-start.7 = (f32[16,512]{1,0:T(8,128)S(1)}, f32[16,512]{1,0:T(8,128)S(1)}, u32[]{:S(2)}, u32[]{:S(2)}) collective-permute-start(f32[16,512]{1,0:T(8,128)S(1)} %multiply_add_fusion.1), channel_id=1, source_target_pairs={{0,192},{16,208},{32,224},{48,240},{64,256},{80,272},{96,288},{112... | collective-permute-start | bytes 98312 | tf_op jit(solution)/shard_map/ppermute | solution.py:16
  56.5 4.0 %collective-permute-start.8 = (f32[16,512]{1,0:T(8,128)S(1)}, f32[16,512]{1,0:T(8,128)S(1)}, u32[]{:S(2)}, u32[]{:S(2)}) collective-permute-start(f32[16,512]{1,0:T(8,128)S(1)} %multiply_add_fusion), channel_id=1, source_target_pairs={{0,256},{16,272},{32,288},{48,304},{64,320},{80,336},{96,352},{112... | collective-permute-start | bytes 98312 | tf_op jit(solution)/shard_map/ppermute | solution.py:16
  64.0 6.5 %multiply_reduce_fusion.2 = f32[256,512]{1,0:T(8,128)S(1)} fusion(f32[16,512]{1,0:T(8,128)S(1)} %neg.6, f32[16,512]{1,0:T(8,128)S(1)} %get-tuple-element.6, f32[16,512,256]{2,1,0:T(8,128)S(1)} %bitcast.113), kind=kOutput, calls=%fused_computation.3 | convolution fusion | flops 6450774016 | bytes 8978432 | tf_op jit(solution)/shard_map/dot_general | solution.py:105
  70.9 2.5 %collective-permute-start.9 = (bf16[256,512]{1,0:T(8,128)(2,1)S(1)}, bf16[256,512]{1,0:T(8,128)(2,1)S(1)}, u32[]{:S(2)}, u32[]{:S(2)}) collective-permute-start(bf16[256,512]{1,0:T(8,128)(2,1)S(1)} %fusion.29), channel_id=1, source_target_pairs={{0,8},{1,9},{2,10},{3,11},{4,12},{5,13},{6,14},{7,15},{8,0},{9,1},... | collective-permute-start | bytes 786440 | tf_op jit(solution)/shard_map/ppermute | solution.py:20
  73.7 13.0 %collective-permute-done.9 = bf16[256,512]{1,0:T(8,128)(2,1)S(1)} collective-permute-done((bf16[256,512]{1,0:T(8,128)(2,1)S(1)}, bf16[256,512]{1,0:T(8,128)(2,1)S(1)}, u32[]{:S(2)}, u32[]{:S(2)}) %collective-permute-start.9) | collective-permute-done | bytes 262176 | tf_op jit(solution)/shard_map/ppermute | solution.py:20
  86.9 3.5 %collective-permute-start.13 = (bf16[2,256,512]{2,1,0:T(8,128)(2,1)S(1)}, bf16[2,256,512]{2,1,0:T(8,128)(2,1)S(1)}, u32[]{:S(2)}, u32[]{:S(2)}) collective-permute-start(bf16[2,256,512]{2,1,0:T(8,128)(2,1)S(1)} %maximum_select_fusion), channel_id=1, source_target_pairs={{0,1},{1,2},{2,3},{3,4},{4,5},{5,6},{6,7},{7,0},{8,9},{9,10},{10,1... | collective-permute-start | bytes 1572872 | tf_op jit(solution)/shard_map/ppermute | solution.py:20
  90.4 3.5 %collective-permute-start.10 = (bf16[2,256,512]{2,1,0:T(8,128)(2,1)S(1)}, bf16[2,256,512]{2,1,0:T(8,128)(2,1)S(1)}, u32[]{:S(2)}, u32[]{:S(2)}) collective-permute-start(bf16[2,256,512]{2,1,0:T(8,128)(2,1)S(1)} %maximum_select_fusion), channel_id=1, source_target_pairs={{0,7},{1,0},{2,1},{3,2},{4,3},{5,4},{6,5},{7,6},{8,15},{9,8},{10,9... | collective-permute-start | bytes 1572872 | tf_op jit(solution)/shard_map/ppermute | solution.py:20
  93.9 7.5 %collective-permute-done.13 = bf16[2,256,512]{2,1,0:T(8,128)(2,1)S(1)} collective-permute-done((bf16[2,256,512]{2,1,0:T(8,128)(2,1)S(1)}, bf16[2,256,512]{2,1,0:T(8,128)(2,1)S(1)}, u32[]{:S(2)}, u32[]{:S(2)}) %collective-permute-start.13) | collective-permute-done | bytes 524320 | tf_op jit(solution)/shard_map/ppermute | solution.py:20
  101.4 1.9 %collective-permute-start.14 = (bf16[2,256,512]{2,1,0:T(8,128)(2,1)S(1)}, bf16[2,256,512]{2,1,0:T(8,128)(2,1)S(1)}, u32[]{:S(2)}, u32[]{:S(2)}) collective-permute-start(bf16[2,256,512]{2,1,0:T(8,128)(2,1)S(1)} %collective-permute-done.13), channel_id=1, source_target_pairs={{0,1},{1,2},{2,3},{3,4},{4,5},{5,6},{6,7},{7,0},{8,9},{9,10},{10,1... | collective-permute-start | bytes 1572872 | tf_op jit(solution)/shard_map/ppermute | solution.py:20
  103.3 5.1 %collective-permute-start.11 = (bf16[2,256,512]{2,1,0:T(8,128)(2,1)S(1)}, bf16[2,256,512]{2,1,0:T(8,128)(2,1)}, u32[]{:S(2)}, u32[]{:S(2)}) collective-permute-start(bf16[2,256,512]{2,1,0:T(8,128)(2,1)S(1)} %collective-permute-done.10), channel_id=1, source_target_pairs={{0,7},{1,0},{2,1},{3,2},{4,3},{5,4},{6,5},{7,6},{8,15},{9,8},{10,9... | collective-permute-start | bytes 1572872 | tf_op jit(solution)/shard_map/ppermute | solution.py:20
  108.5 6.6 %collective-permute-done.14 = bf16[2,256,512]{2,1,0:T(8,128)(2,1)S(1)} collective-permute-done((bf16[2,256,512]{2,1,0:T(8,128)(2,1)S(1)}, bf16[2,256,512]{2,1,0:T(8,128)(2,1)S(1)}, u32[]{:S(2)}, u32[]{:S(2)}) %collective-permute-start.14) | collective-permute-done | bytes 524320 | tf_op jit(solution)/shard_map/ppermute | solution.py:20
  115.1 1.9 %collective-permute-start.15 = (bf16[2,256,512]{2,1,0:T(8,128)(2,1)S(1)}, bf16[2,256,512]{2,1,0:T(8,128)(2,1)S(1)}, u32[]{:S(2)}, u32[]{:S(2)}) collective-permute-start(bf16[2,256,512]{2,1,0:T(8,128)(2,1)S(1)} %collective-permute-done.14), channel_id=1, source_target_pairs={{0,1},{1,2},{2,3},{3,4},{4,5},{5,6},{6,7},{7,0},{8,9},{9,10},{10,1... | collective-permute-start | bytes 1572872 | tf_op jit(solution)/shard_map/ppermute | solution.py:20
  117.0 5.1 %collective-permute-start.12 = (bf16[2,256,512]{2,1,0:T(8,128)(2,1)}, bf16[2,256,512]{2,1,0:T(8,128)(2,1)S(1)}, u32[]{:S(2)}, u32[]{:S(2)}) collective-permute-start(bf16[2,256,512]{2,1,0:T(8,128)(2,1)} %collective-permute-done.11), channel_id=1, source_target_pairs={{0,7},{1,0},{2,1},{3,2},{4,3},{5,4},{6,5},{7,6},{8,15},{9,8},{10,9... | collective-permute-start | bytes 1572872 | tf_op jit(solution)/shard_map/ppermute | solution.py:20
  122.3 5.6 %collective-permute-done.15 = bf16[2,256,512]{2,1,0:T(8,128)(2,1)S(1)} collective-permute-done((bf16[2,256,512]{2,1,0:T(8,128)(2,1)S(1)}, bf16[2,256,512]{2,1,0:T(8,128)(2,1)S(1)}, u32[]{:S(2)}, u32[]{:S(2)}) %collective-permute-start.15) | collective-permute-done | bytes 524320 | tf_op jit(solution)/shard_map/ppermute | solution.py:20
  127.9 1.9 %collective-permute-start.16 = (bf16[1,256,512]{2,1,0:T(8,128)(2,1)S(1)}, bf16[1,256,512]{2,1,0:T(8,128)(2,1)}, u32[]{:S(2)}, u32[]{:S(2)}) collective-permute-start(bf16[1,256,512]{2,1,0:T(8,128)(2,1)S(1)} %slice.54), channel_id=1, source_target_pairs={{0,1},{1,2},{2,3},{3,4},{4,5},{5,6},{6,7},{7,0},{8,9},{9,10},{10,1... | collective-permute-start | bytes 786440 | tf_op jit(solution)/shard_map/ppermute | solution.py:20
  130.6 5.1 %collective-permute-start.17 = (bf16[1,256,512]{2,1,0:T(8,128)(2,1)}, bf16[1,256,512]{2,1,0:T(8,128)(2,1)}, u32[]{:S(2)}, u32[]{:S(2)}) collective-permute-start(bf16[1,256,512]{2,1,0:T(8,128)(2,1)} %slice.55), channel_id=1, source_target_pairs={{0,7},{1,0},{2,1},{3,2},{4,3},{5,4},{6,5},{7,6},{8,15},{9,8},{10,9... | collective-permute-start | bytes 786440 | tf_op jit(solution)/shard_map/ppermute | solution.py:20
  135.8 1.8 %convolution_bitcast_fusion.6 = f32[256,512]{1,0:T(8,128)S(1)} fusion(bf16[2,256,512]{2,1,0:T(8,128)(2,1)S(1)} %collective-permute-done.10, bf16[2,8,512,512]{3,2,1,0:T(8,128)(2,1)} %bitcast.114, s32[]{:T(128)S(6)} %select_n.83), kind=kOutput, calls=%fused_computation.15 | convolution fusion | flops 268435456 | bytes 2097156 | tf_op jit(solution)/shard_map/htc,hco->to/dot_general | solution.py:127
  137.6 2.1 %fusion.2 = f32[256,512]{1,0:T(8,128)S(1)} fusion(f32[256,512]{1,0:T(8,128)S(1)} %convolution_bitcast_fusion.6, bf16[2,256,512]{2,1,0:T(8,128)(2,1)S(1)} %maximum_select_fusion, bf16[2,8,512,512]{3,2,1,0:T(8,128)(2,1)} %bitcast.115, s32[]{:T(128)S(6)} %select_n.81), kind=kOutput, calls=%fused_computation.17 | convolution fusion | flops 268566528 | bytes 2621444 | tf_op jit(solution)/shard_map/htc,hco->to/dot_general | solution.py:127
  (55 shorter events, 24.4 us)
Async XLA Ops:
  6.5 30.3 %copy-start.1 = (f32[16,512]{1,0:T(8,128)S(1)}, f32[16,512]{1,0:T(8,128)}, u32[]{:S(2)}) copy-start(f32[16,512]{1,0:T(8,128)} %param.8) | copy-start | bytes 98308
  6.5 129.2 %all-gather.2.cloned.1.call-start = ((), (), s32[]{:S(2)}) async-start(), calls=%async_computation | async-start | bytes 8650752 | tf_op jit(solution)/shard_map/all_gather | solution.py:119
  8.0 3.4 %collective-permute-start = (bf16[3,2,512]{2,1,0:T(2,128)(2,1)S(1)}, bf16[3,2,512]{2,1,0:T(2,128)(2,1)S(1)}, u32[]{:S(2)}, u32[]{:S(2)}) collective-permute-start(bf16[3,2,512]{2,1,0:T(2,128)(2,1)S(1)} %slice.37), channel_id=1, source_target_pairs={{0,16},{16,32},{32,48},{48,64},{64,80},{80,96},{96,112},{112,128},... | collective-permute-start | bytes 18440 | tf_op jit(solution)/shard_map/ppermute | solution.py:16
  13.3 49.2 %copy-start.2 = (f32[16,512]{1,0:T(8,128)S(1)}, f32[16,512]{1,0:T(8,128)}, u32[]{:S(2)}) copy-start(f32[16,512]{1,0:T(8,128)} %param.9) | copy-start | bytes 98308
  14.9 20.3 %collective-permute-start.1 = (f32[16,512]{1,0:T(8,128)S(1)}, f32[16,512]{1,0:T(8,128)S(1)}, u32[]{:S(2)}, u32[]{:S(2)}) collective-permute-start(f32[16,512]{1,0:T(8,128)S(1)} %multiply_reduce_fusion.1), channel_id=1, source_target_pairs={{0,16},{16,32},{32,48},{48,64},{64,80},{80,96},{96,112},{112,128},... | collective-permute-start | bytes 98312 | tf_op jit(solution)/shard_map/ppermute | solution.py:16
  19.4 15.7 %collective-permute-start.2 = (f32[16,512]{1,0:T(8,128)S(1)}, f32[16,512]{1,0:T(8,128)S(1)}, u32[]{:S(2)}, u32[]{:S(2)}) collective-permute-start(f32[16,512]{1,0:T(8,128)S(1)} %multiply_reduce_fusion.1), channel_id=1, source_target_pairs={{0,32},{16,48},{32,64},{48,80},{64,96},{80,112},{96,128},{112,144}... | collective-permute-start | bytes 98312 | tf_op jit(solution)/shard_map/ppermute | solution.py:16
  23.7 11.4 %collective-permute-start.3 = (f32[16,512]{1,0:T(8,128)S(1)}, f32[16,512]{1,0:T(8,128)S(1)}, u32[]{:S(2)}, u32[]{:S(2)}) collective-permute-start(f32[16,512]{1,0:T(8,128)S(1)} %multiply_reduce_fusion.1), channel_id=1, source_target_pairs={{0,48},{16,64},{32,80},{48,96},{64,112},{80,128},{96,144},{112,160... | collective-permute-start | bytes 98312 | tf_op jit(solution)/shard_map/ppermute | solution.py:16
  28.7 8.2 %collective-permute-start.4 = (f32[16,512]{1,0:T(8,128)S(1)}, f32[16,512]{1,0:T(8,128)S(1)}, u32[]{:S(2)}, u32[]{:S(2)}) collective-permute-start(f32[16,512]{1,0:T(8,128)S(1)} %multiply_reduce_fusion.1), channel_id=1, source_target_pairs={{0,64},{16,80},{32,96},{48,112},{64,128},{80,144},{96,160},{112,17... | collective-permute-start | bytes 98312 | tf_op jit(solution)/shard_map/ppermute | solution.py:16
  36.9 18.0 %collective-permute-start.5 = (f32[16,512]{1,0:T(8,128)S(1)}, f32[16,512]{1,0:T(8,128)S(1)}, u32[]{:S(2)}, u32[]{:S(2)}) collective-permute-start(f32[16,512]{1,0:T(8,128)S(1)} %multiply_add_fusion.1), channel_id=1, source_target_pairs={{0,64},{16,80},{32,96},{48,112},{64,128},{80,144},{96,160},{112,17... | collective-permute-start | bytes 98312 | tf_op jit(solution)/shard_map/ppermute | solution.py:16
  42.2 12.8 %collective-permute-start.6 = (f32[16,512]{1,0:T(8,128)S(1)}, f32[16,512]{1,0:T(8,128)S(1)}, u32[]{:S(2)}, u32[]{:S(2)}) collective-permute-start(f32[16,512]{1,0:T(8,128)S(1)} %multiply_add_fusion.1), channel_id=1, source_target_pairs={{0,128},{16,144},{32,160},{48,176},{64,192},{80,208},{96,224},{112... | collective-permute-start | bytes 98312 | tf_op jit(solution)/shard_map/ppermute | solution.py:16
  48.0 8.6 %collective-permute-start.7 = (f32[16,512]{1,0:T(8,128)S(1)}, f32[16,512]{1,0:T(8,128)S(1)}, u32[]{:S(2)}, u32[]{:S(2)}) collective-permute-start(f32[16,512]{1,0:T(8,128)S(1)} %multiply_add_fusion.1), channel_id=1, source_target_pairs={{0,192},{16,208},{32,224},{48,240},{64,256},{80,272},{96,288},{112... | collective-permute-start | bytes 98312 | tf_op jit(solution)/shard_map/ppermute | solution.py:16
  56.5 6.0 %collective-permute-start.8 = (f32[16,512]{1,0:T(8,128)S(1)}, f32[16,512]{1,0:T(8,128)S(1)}, u32[]{:S(2)}, u32[]{:S(2)}) collective-permute-start(f32[16,512]{1,0:T(8,128)S(1)} %multiply_add_fusion), channel_id=1, source_target_pairs={{0,256},{16,272},{32,288},{48,304},{64,320},{80,336},{96,352},{112... | collective-permute-start | bytes 98312 | tf_op jit(solution)/shard_map/ppermute | solution.py:16
  62.1 8.5 %copy-start.3 = (f32[512]{0:T(512)S(1)}, f32[512]{0:T(512)}, u32[]{:S(2)}) copy-start(f32[512]{0:T(512)} %param.10) | copy-start | bytes 6148
  70.9 15.9 %collective-permute-start.9 = (bf16[256,512]{1,0:T(8,128)(2,1)S(1)}, bf16[256,512]{1,0:T(8,128)(2,1)S(1)}, u32[]{:S(2)}, u32[]{:S(2)}) collective-permute-start(bf16[256,512]{1,0:T(8,128)(2,1)S(1)} %fusion.29), channel_id=1, source_target_pairs={{0,8},{1,9},{2,10},{3,11},{4,12},{5,13},{6,14},{7,15},{8,0},{9,1},... | collective-permute-start | bytes 786440 | tf_op jit(solution)/shard_map/ppermute | solution.py:20
  86.9 14.5 %collective-permute-start.13 = (bf16[2,256,512]{2,1,0:T(8,128)(2,1)S(1)}, bf16[2,256,512]{2,1,0:T(8,128)(2,1)S(1)}, u32[]{:S(2)}, u32[]{:S(2)}) collective-permute-start(bf16[2,256,512]{2,1,0:T(8,128)(2,1)S(1)} %maximum_select_fusion), channel_id=1, source_target_pairs={{0,1},{1,2},{2,3},{3,4},{4,5},{5,6},{6,7},{7,0},{8,9},{9,10},{10,1... | collective-permute-start | bytes 1572872 | tf_op jit(solution)/shard_map/ppermute | solution.py:20
  90.4 12.9 %collective-permute-start.10 = (bf16[2,256,512]{2,1,0:T(8,128)(2,1)S(1)}, bf16[2,256,512]{2,1,0:T(8,128)(2,1)S(1)}, u32[]{:S(2)}, u32[]{:S(2)}) collective-permute-start(bf16[2,256,512]{2,1,0:T(8,128)(2,1)S(1)} %maximum_select_fusion), channel_id=1, source_target_pairs={{0,7},{1,0},{2,1},{3,2},{4,3},{5,4},{6,5},{7,6},{8,15},{9,8},{10,9... | collective-permute-start | bytes 1572872 | tf_op jit(solution)/shard_map/ppermute | solution.py:20
  101.4 13.7 %collective-permute-start.14 = (bf16[2,256,512]{2,1,0:T(8,128)(2,1)S(1)}, bf16[2,256,512]{2,1,0:T(8,128)(2,1)S(1)}, u32[]{:S(2)}, u32[]{:S(2)}) collective-permute-start(bf16[2,256,512]{2,1,0:T(8,128)(2,1)S(1)} %collective-permute-done.13), channel_id=1, source_target_pairs={{0,1},{1,2},{2,3},{3,4},{4,5},{5,6},{6,7},{7,0},{8,9},{9,10},{10,1... | collective-permute-start | bytes 1572872 | tf_op jit(solution)/shard_map/ppermute | solution.py:20
  103.3 13.7 %collective-permute-start.11 = (bf16[2,256,512]{2,1,0:T(8,128)(2,1)S(1)}, bf16[2,256,512]{2,1,0:T(8,128)(2,1)}, u32[]{:S(2)}, u32[]{:S(2)}) collective-permute-start(bf16[2,256,512]{2,1,0:T(8,128)(2,1)S(1)} %collective-permute-done.10), channel_id=1, source_target_pairs={{0,7},{1,0},{2,1},{3,2},{4,3},{5,4},{6,5},{7,6},{8,15},{9,8},{10,9... | collective-permute-start | bytes 1572872 | tf_op jit(solution)/shard_map/ppermute | solution.py:20
  115.1 12.8 %collective-permute-start.15 = (bf16[2,256,512]{2,1,0:T(8,128)(2,1)S(1)}, bf16[2,256,512]{2,1,0:T(8,128)(2,1)S(1)}, u32[]{:S(2)}, u32[]{:S(2)}) collective-permute-start(bf16[2,256,512]{2,1,0:T(8,128)(2,1)S(1)} %collective-permute-done.14), channel_id=1, source_target_pairs={{0,1},{1,2},{2,3},{3,4},{4,5},{5,6},{6,7},{7,0},{8,9},{9,10},{10,1... | collective-permute-start | bytes 1572872 | tf_op jit(solution)/shard_map/ppermute | solution.py:20
  117.0 12.8 %collective-permute-start.12 = (bf16[2,256,512]{2,1,0:T(8,128)(2,1)}, bf16[2,256,512]{2,1,0:T(8,128)(2,1)S(1)}, u32[]{:S(2)}, u32[]{:S(2)}) collective-permute-start(bf16[2,256,512]{2,1,0:T(8,128)(2,1)} %collective-permute-done.11), channel_id=1, source_target_pairs={{0,7},{1,0},{2,1},{3,2},{4,3},{5,4},{6,5},{7,6},{8,15},{9,8},{10,9... | collective-permute-start | bytes 1572872 | tf_op jit(solution)/shard_map/ppermute | solution.py:20
  127.9 17.0 %collective-permute-start.16 = (bf16[1,256,512]{2,1,0:T(8,128)(2,1)S(1)}, bf16[1,256,512]{2,1,0:T(8,128)(2,1)}, u32[]{:S(2)}, u32[]{:S(2)}) collective-permute-start(bf16[1,256,512]{2,1,0:T(8,128)(2,1)S(1)} %slice.54), channel_id=1, source_target_pairs={{0,1},{1,2},{2,3},{3,4},{4,5},{5,6},{6,7},{7,0},{8,9},{9,10},{10,1... | collective-permute-start | bytes 786440 | tf_op jit(solution)/shard_map/ppermute | solution.py:20
  130.6 14.4 %collective-permute-start.17 = (bf16[1,256,512]{2,1,0:T(8,128)(2,1)}, bf16[1,256,512]{2,1,0:T(8,128)(2,1)}, u32[]{:S(2)}, u32[]{:S(2)}) collective-permute-start(bf16[1,256,512]{2,1,0:T(8,128)(2,1)} %slice.55), channel_id=1, source_target_pairs={{0,7},{1,0},{2,1},{3,2},{4,3},{5,4},{6,5},{7,6},{8,15},{9,8},{10,9... | collective-permute-start | bytes 786440 | tf_op jit(solution)/shard_map/ppermute | solution.py:20
  135.7 7.3 %copy-start = (bf16[8192,512]{1,0:T(8,128)(2,1)S(1)}, bf16[8192,512]{1,0:T(8,128)(2,1)}, u32[]{:S(2)}) copy-start(bf16[8192,512]{1,0:T(8,128)(2,1)} %all-gather.2.cloned.1.call-done) | copy-start | bytes 25165828
Sparse Core Ops, SparseCore 0:
  9.5 84.2 all-gather.1

commit v4 on v1

--- a/solution.py
+++ b/solution.py
@@ -109,7 +109,10 @@
 def tail(mixed_local, out_weight):
     channels = mixed_local.shape[1]
     features = ring_gather(mixed_local, "tensor", 8)
-    weight_all = lax.all_gather(out_weight, "seq", axis=0, tiled=True)
+    sections = lax.axis_size("seq")
+    spread = jnp.broadcast_to(out_weight[None], (sections,) + out_weight.shape)
+    weight_all = lax.all_to_all(spread, "seq", 0, 0)
+    weight_all = weight_all.reshape(sections * out_weight.shape[0], out_weight.shape[1])
     ring = len(features)
     halves = features[0].shape[0]
     weight_all = weight_all.reshape(halves, ring, channels, weight_all.shape[1])

time: 151 us -> 319 us (2.11)
  waiting for transfers between devices: 52 us -> 216 us
  between operations: 14 us -> 0.64 us
  starting transfers between devices: 56.6 us -> 68.9 us
  local copies, waits for them, and re-layouts: 1.86 us -> 5.4 us
    ppermute x9, waiting for transfers between devices: 22.8 us -> 194 us  [passed_along(): return lax.ppermute(block, axis, route)]
    all_to_all x0 -> x1, starting transfers between devices: none -> 12.1 us  [tail(): weight_all = lax.all_to_all(spread, 'seq', 0, 0)]
    ppermute x8, waiting for transfers between devices: 28.4 us -> 21.9 us  [shifted(): return lax.ppermute(block, axis, route)]
    broadcast_in_dim x0 -> x1, local copies, waits for them, and re-layouts: none -> 5.14 us  [tail(): spread = jnp.broadcast_to(out_weight[None], (sections,) + out_weight.shape)]
  transfers between devices with their start and end apart: 18 -> 18, of which waited for: 10 -> 10; matrix products, arithmetic and copies ran while one was open for 18% -> 8% of each run, Pallas kernels for 0% -> 0%
where the time goes in v4:
time: 319 us; the launch traced here: 318 us
  waiting for transfers between devices  216 us (68%)
  starting transfers between devices  68.9 us (22%)
  matrix products  20.9 us (7%)
  other arithmetic  5.77 us (2%)
  local copies, waits for them, and re-layouts  5.4 us (2%)
    ppermute x9, waiting for transfers between devices, passed_along(): return lax.ppermute(block, axis, route)  194 us
    ppermute x8, starting transfers between devices, shifted(): return lax.ppermute(block, axis, route)  31.3 us
    ppermute x9, starting transfers between devices, passed_along(): return lax.ppermute(block, axis, route)  25.5 us
    ppermute x8, waiting for transfers between devices, shifted(): return lax.ppermute(block, axis, route)  21.9 us
    dot_general x8, matrix products, tail(): jnp.einsum('htc,hco->to', features[r], taken, preferred_element_type=jnp....  14.4 us
    all_to_all x1, starting transfers between devices, tail(): weight_all = lax.all_to_all(spread, 'seq', 0, 0)  12.1 us
    dot_general x1, matrix products, finish(): jnp.dot(lower, scaled, precision=PRECISE)  6.54 us
  transfers between devices with their start and end apart: 18, of which 10 were waited for; matrix products, arithmetic and copies ran while one was open for 8% of the time, Pallas kernels for 0%

profile of v4, /device:TPU:26, one launch (start us, length us, event | category | flops | bytes accessed | tf_op | source)
XLA Modules:
  0.0 317.6 jit_solution(14301200229684024836)
XLA Ops:
  0.0 5.1 %broadcast_in_dim.2 = bf16[32,256,512]{2,1,0:T(8,128)(2,1)} broadcast(bf16[256,512]{1,0:T(8,128)(2,1)} %param.11), dimensions={1,2} | broadcast | bytes 8650752 | tf_op jit(solution)/shard_map/broadcast_in_dim | solution.py:113
  5.1 12.1 %all-to-all-start = ((bf16[32,256,512]{2,1,0:T(8,128)(2,1)}), bf16[32,256,512]{2,1,0:T(8,128)(2,1)}, u32[]{:S(2)}, u32[]{:S(2)}) async-start(bf16[32,256,512]{2,1,0:T(8,128)(2,1)} %broadcast_in_dim.2), calls=%async_computation | async-start | bytes 16777216 | tf_op jit(solution)/shard_map/all_to_all | solution.py:114
  17.3 2.0 collective-permute-start
  19.4 180.0 %collective-permute-done = bf16[3,2,512]{2,1,0:T(2,128)(2,1)S(1)} collective-permute-done((bf16[3,2,512]{2,1,0:T(2,128)(2,1)S(1)}, bf16[3,2,512]{2,1,0:T(2,128)(2,1)S(1)}, u32[]{:S(2)}, u32[]{:S(2)}) %collective-permute-start) | collective-permute-done | bytes 6176 | tf_op jit(solution)/shard_map/ppermute | solution.py:16
  203.6 2.7 collective-permute-start.2
  206.3 5.5 %collective-permute-start.3 = (f32[16,512]{1,0:T(8,128)S(1)}, f32[16,512]{1,0:T(8,128)S(1)}, u32[]{:S(2)}, u32[]{:S(2)}) collective-permute-start(f32[16,512]{1,0:T(8,128)S(1)} %multiply_reduce_fusion.1), channel_id=1, source_target_pairs={{0,48},{16,64},{32,80},{48,96},{64,112},{80,128},{96,144},{112,160... | collective-permute-start | bytes 98312 | tf_op jit(solution)/shard_map/ppermute | solution.py:16
  211.8 4.2 %collective-permute-start.4 = (f32[16,512]{1,0:T(8,128)S(1)}, f32[16,512]{1,0:T(8,128)S(1)}, u32[]{:S(2)}, u32[]{:S(2)}) collective-permute-start(f32[16,512]{1,0:T(8,128)S(1)} %multiply_reduce_fusion.1), channel_id=1, source_target_pairs={{0,64},{16,80},{32,96},{48,112},{64,128},{80,144},{96,160},{112,17... | collective-permute-start | bytes 98312 | tf_op jit(solution)/shard_map/ppermute | solution.py:16
  216.1 4.7 %collective-permute-done.4 = f32[16,512]{1,0:T(8,128)S(1)} collective-permute-done((f32[16,512]{1,0:T(8,128)S(1)}, f32[16,512]{1,0:T(8,128)S(1)}, u32[]{:S(2)}, u32[]{:S(2)}) %collective-permute-start.4) | collective-permute-done | bytes 32800 | tf_op jit(solution)/shard_map/ppermute | solution.py:16
  220.8 1.9 collective-permute-start.5
  222.8 4.1 %collective-permute-start.6 = (f32[16,512]{1,0:T(8,128)S(1)}, f32[16,512]{1,0:T(8,128)S(1)}, u32[]{:S(2)}, u32[]{:S(2)}) collective-permute-start(f32[16,512]{1,0:T(8,128)S(1)} %multiply_add_fusion.1), channel_id=1, source_target_pairs={{0,128},{16,144},{32,160},{48,176},{64,192},{80,208},{96,224},{112... | collective-permute-start | bytes 98312 | tf_op jit(solution)/shard_map/ppermute | solution.py:16
  229.6 3.8 %collective-permute-done.6 = f32[16,512]{1,0:T(8,128)S(1)} collective-permute-done((f32[16,512]{1,0:T(8,128)S(1)}, f32[16,512]{1,0:T(8,128)S(1)}, u32[]{:S(2)}, u32[]{:S(2)}) %collective-permute-start.6) | collective-permute-done | bytes 32800 | tf_op jit(solution)/shard_map/ppermute | solution.py:16
  238.1 3.0 collective-permute-done.8
  242.5 6.5 %multiply_reduce_fusion.2 = f32[256,512]{1,0:T(8,128)S(1)} fusion(f32[16,512]{1,0:T(8,128)S(1)} %neg.6, f32[16,512]{1,0:T(8,128)S(1)} %get-tuple-element.6, f32[16,512,256]{2,1,0:T(8,128)S(1)} %bitcast.98), kind=kOutput, calls=%fused_computation.3 | convolution fusion | flops 6450774016 | bytes 8978432 | tf_op jit(solution)/shard_map/dot_general | solution.py:98
  249.4 4.0 %collective-permute-start.9 = (bf16[256,512]{1,0:T(8,128)(2,1)S(1)}, bf16[256,512]{1,0:T(8,128)(2,1)S(1)}, u32[]{:S(2)}, u32[]{:S(2)}) collective-permute-start(bf16[256,512]{1,0:T(8,128)(2,1)S(1)} %fusion.26), channel_id=1, source_target_pairs={{0,8},{1,9},{2,10},{3,11},{4,12},{5,13},{6,14},{7,15},{8,0},{9,1},... | collective-permute-start | bytes 786440 | tf_op jit(solution)/shard_map/ppermute | solution.py:20
  253.8 5.4 %collective-permute-done.9 = bf16[256,512]{1,0:T(8,128)(2,1)S(1)} collective-permute-done((bf16[256,512]{1,0:T(8,128)(2,1)S(1)}, bf16[256,512]{1,0:T(8,128)(2,1)S(1)}, u32[]{:S(2)}, u32[]{:S(2)}) %collective-permute-start.9) | collective-permute-done | bytes 262176 | tf_op jit(solution)/shard_map/ppermute | solution.py:20
  259.2 4.7 %collective-permute-start.13 = (bf16[2,256,512]{2,1,0:T(8,128)(2,1)S(1)}, bf16[2,256,512]{2,1,0:T(8,128)(2,1)S(1)}, u32[]{:S(2)}, u32[]{:S(2)}) collective-permute-start(bf16[2,256,512]{2,1,0:T(8,128)(2,1)S(1)} %maximum_select_fusion), channel_id=1, source_target_pairs={{0,1},{1,2},{2,3},{3,4},{4,5},{5,6},{6,7},{7,0},{8,9},{9,10},{10,1... | collective-permute-start | bytes 1572872 | tf_op jit(solution)/shard_map/ppermute | solution.py:20
  265.9 5.4 %collective-permute-done.13 = bf16[2,256,512]{2,1,0:T(8,128)(2,1)S(1)} collective-permute-done((bf16[2,256,512]{2,1,0:T(8,128)(2,1)S(1)}, bf16[2,256,512]{2,1,0:T(8,128)(2,1)S(1)}, u32[]{:S(2)}, u32[]{:S(2)}) %collective-permute-start.13) | collective-permute-done | bytes 524320 | tf_op jit(solution)/shard_map/ppermute | solution.py:20
  271.3 5.6 %collective-permute-start.14 = (bf16[2,256,512]{2,1,0:T(8,128)(2,1)S(1)}, bf16[2,256,512]{2,1,0:T(8,128)(2,1)S(1)}, u32[]{:S(2)}, u32[]{:S(2)}) collective-permute-start(bf16[2,256,512]{2,1,0:T(8,128)(2,1)S(1)} %collective-permute-done.13), channel_id=1, source_target_pairs={{0,1},{1,2},{2,3},{3,4},{4,5},{5,6},{6,7},{7,0},{8,9},{9,10},{10,1... | collective-permute-start | bytes 1572872 | tf_op jit(solution)/shard_map/ppermute | solution.py:20
  276.9 1.9 collective-permute-start.11
  278.9 5.0 %collective-permute-done.14 = bf16[2,256,512]{2,1,0:T(8,128)(2,1)S(1)} collective-permute-done((bf16[2,256,512]{2,1,0:T(8,128)(2,1)S(1)}, bf16[2,256,512]{2,1,0:T(8,128)(2,1)S(1)}, u32[]{:S(2)}, u32[]{:S(2)}) %collective-permute-start.14) | collective-permute-done | bytes 524320 | tf_op jit(solution)/shard_map/ppermute | solution.py:20
  283.9 5.6 %collective-permute-start.15 = (bf16[2,256,512]{2,1,0:T(8,128)(2,1)S(1)}, bf16[2,256,512]{2,1,0:T(8,128)(2,1)S(1)}, u32[]{:S(2)}, u32[]{:S(2)}) collective-permute-start(bf16[2,256,512]{2,1,0:T(8,128)(2,1)S(1)} %collective-permute-done.14), channel_id=1, source_target_pairs={{0,1},{1,2},{2,3},{3,4},{4,5},{5,6},{6,7},{7,0},{8,9},{9,10},{10,1... | collective-permute-start | bytes 1572872 | tf_op jit(solution)/shard_map/ppermute | solution.py:20
  291.6 6.0 %collective-permute-done.15 = bf16[2,256,512]{2,1,0:T(8,128)(2,1)S(1)} collective-permute-done((bf16[2,256,512]{2,1,0:T(8,128)(2,1)S(1)}, bf16[2,256,512]{2,1,0:T(8,128)(2,1)S(1)}, u32[]{:S(2)}, u32[]{:S(2)}) %collective-permute-start.15) | collective-permute-done | bytes 524320 | tf_op jit(solution)/shard_map/ppermute | solution.py:20
  297.6 5.6 %collective-permute-start.16 = (bf16[2,256,512]{2,1,0:T(8,128)(2,1)S(1)}, bf16[2,256,512]{2,1,0:T(8,128)(2,1)S(1)}, u32[]{:S(2)}, u32[]{:S(2)}) collective-permute-start(bf16[2,256,512]{2,1,0:T(8,128)(2,1)S(1)} %collective-permute-done.15), channel_id=1, source_target_pairs={{0,1},{1,2},{2,3},{3,4},{4,5},{5,6},{6,7},{7,0},{8,9},{9,10},{10,1... | collective-permute-start | bytes 1572872 | tf_op jit(solution)/shard_map/ppermute | solution.py:20
  315.2 2.4 fusion.9
  (53 shorter events, 29.6 us)
Async XLA Ops:
  5.1 12.1 %copy-start.1 = (bf16[3,256,512]{2,1,0:T(8,128)(2,1)S(1)}, bf16[3,256,512]{2,1,0:T(8,128)(2,1)}, u32[]{:S(2)}) copy-start(bf16[3,256,512]{2,1,0:T(8,128)(2,1)} %param.6) | copy-start | bytes 2359300
  5.1 14.2 %copy-start.3 = (f32[3,3,512]{2,1,0:T(4,128)S(1)}, f32[3,3,512]{2,1,0:T(4,128)}, u32[]{:S(2)}) copy-start(f32[3,3,512]{2,1,0:T(4,128)} %param.7) | copy-start | bytes 55300
  5.1 14.3 %copy-start = (f32[16,512]{1,0:T(8,128)S(1)}, f32[16,512]{1,0:T(8,128)}, u32[]{:S(2)}) copy-start(f32[16,512]{1,0:T(8,128)} %param.8) | copy-start | bytes 98308
  5.1 298.0 %all-to-all-start = ((bf16[32,256,512]{2,1,0:T(8,128)(2,1)}), bf16[32,256,512]{2,1,0:T(8,128)(2,1)}, u32[]{:S(2)}, u32[]{:S(2)}) async-start(bf16[32,256,512]{2,1,0:T(8,128)(2,1)} %broadcast_in_dim.2), calls=%async_computation | async-start | bytes 16777216 | tf_op jit(solution)/shard_map/all_to_all | solution.py:114
  17.3 182.1 %collective-permute-start = (bf16[3,2,512]{2,1,0:T(2,128)(2,1)S(1)}, bf16[3,2,512]{2,1,0:T(2,128)(2,1)S(1)}, u32[]{:S(2)}, u32[]{:S(2)}) collective-permute-start(bf16[3,2,512]{2,1,0:T(2,128)(2,1)S(1)} %slice.31), channel_id=1, source_target_pairs={{0,16},{16,32},{32,48},{48,64},{64,80},{80,96},{96,112},{112,128},... | collective-permute-start | bytes 18440 | tf_op jit(solution)/shard_map/ppermute | solution.py:16
  200.1 40.9 %copy-start.2 = (f32[16,512]{1,0:T(8,128)S(1)}, f32[16,512]{1,0:T(8,128)}, u32[]{:S(2)}) copy-start(f32[16,512]{1,0:T(8,128)} %param.9) | copy-start | bytes 98308
  201.7 14.3 %collective-permute-start.1 = (f32[16,512]{1,0:T(8,128)S(1)}, f32[16,512]{1,0:T(8,128)S(1)}, u32[]{:S(2)}, u32[]{:S(2)}) collective-permute-start(f32[16,512]{1,0:T(8,128)S(1)} %multiply_reduce_fusion.1), channel_id=1, source_target_pairs={{0,16},{16,32},{32,48},{48,64},{64,80},{80,96},{96,112},{112,128},... | collective-permute-start | bytes 98312 | tf_op jit(solution)/shard_map/ppermute | solution.py:16
  203.6 12.4 %collective-permute-start.2 = (f32[16,512]{1,0:T(8,128)S(1)}, f32[16,512]{1,0:T(8,128)S(1)}, u32[]{:S(2)}, u32[]{:S(2)}) collective-permute-start(f32[16,512]{1,0:T(8,128)S(1)} %multiply_reduce_fusion.1), channel_id=1, source_target_pairs={{0,32},{16,48},{32,64},{48,80},{64,96},{80,112},{96,128},{112,144}... | collective-permute-start | bytes 98312 | tf_op jit(solution)/shard_map/ppermute | solution.py:16
  206.3 9.7 %collective-permute-start.3 = (f32[16,512]{1,0:T(8,128)S(1)}, f32[16,512]{1,0:T(8,128)S(1)}, u32[]{:S(2)}, u32[]{:S(2)}) collective-permute-start(f32[16,512]{1,0:T(8,128)S(1)} %multiply_reduce_fusion.1), channel_id=1, source_target_pairs={{0,48},{16,64},{32,80},{48,96},{64,112},{80,128},{96,144},{112,160... | collective-permute-start | bytes 98312 | tf_op jit(solution)/shard_map/ppermute | solution.py:16
  211.8 8.9 %collective-permute-start.4 = (f32[16,512]{1,0:T(8,128)S(1)}, f32[16,512]{1,0:T(8,128)S(1)}, u32[]{:S(2)}, u32[]{:S(2)}) collective-permute-start(f32[16,512]{1,0:T(8,128)S(1)} %multiply_reduce_fusion.1), channel_id=1, source_target_pairs={{0,64},{16,80},{32,96},{48,112},{64,128},{80,144},{96,160},{112,17... | collective-permute-start | bytes 98312 | tf_op jit(solution)/shard_map/ppermute | solution.py:16
  220.8 8.8 %collective-permute-start.5 = (f32[16,512]{1,0:T(8,128)S(1)}, f32[16,512]{1,0:T(8,128)S(1)}, u32[]{:S(2)}, u32[]{:S(2)}) collective-permute-start(f32[16,512]{1,0:T(8,128)S(1)} %multiply_add_fusion.1), channel_id=1, source_target_pairs={{0,64},{16,80},{32,96},{48,112},{64,128},{80,144},{96,160},{112,17... | collective-permute-start | bytes 98312 | tf_op jit(solution)/shard_map/ppermute | solution.py:16
  222.8 10.7 %collective-permute-start.6 = (f32[16,512]{1,0:T(8,128)S(1)}, f32[16,512]{1,0:T(8,128)S(1)}, u32[]{:S(2)}, u32[]{:S(2)}) collective-permute-start(f32[16,512]{1,0:T(8,128)S(1)} %multiply_add_fusion.1), channel_id=1, source_target_pairs={{0,128},{16,144},{32,160},{48,176},{64,192},{80,208},{96,224},{112... | collective-permute-start | bytes 98312 | tf_op jit(solution)/shard_map/ppermute | solution.py:16
  226.9 8.3 %collective-permute-start.7 = (f32[16,512]{1,0:T(8,128)S(1)}, f32[16,512]{1,0:T(8,128)S(1)}, u32[]{:S(2)}, u32[]{:S(2)}) collective-permute-start(f32[16,512]{1,0:T(8,128)S(1)} %multiply_add_fusion.1), channel_id=1, source_target_pairs={{0,192},{16,208},{32,224},{48,240},{64,256},{80,272},{96,288},{112... | collective-permute-start | bytes 98312 | tf_op jit(solution)/shard_map/ppermute | solution.py:16
  235.2 5.8 %collective-permute-start.8 = (f32[16,512]{1,0:T(8,128)S(1)}, f32[16,512]{1,0:T(8,128)S(1)}, u32[]{:S(2)}, u32[]{:S(2)}) collective-permute-start(f32[16,512]{1,0:T(8,128)S(1)} %multiply_add_fusion), channel_id=1, source_target_pairs={{0,256},{16,272},{32,288},{48,304},{64,320},{80,336},{96,352},{112... | collective-permute-start | bytes 98312 | tf_op jit(solution)/shard_map/ppermute | solution.py:16
  238.1 11.0 %copy-start.4 = (f32[512]{0:T(512)S(1)}, f32[512]{0:T(512)}, u32[]{:S(2)}) copy-start(f32[512]{0:T(512)} %param.10) | copy-start | bytes 6148
  249.4 9.8 %collective-permute-start.9 = (bf16[256,512]{1,0:T(8,128)(2,1)S(1)}, bf16[256,512]{1,0:T(8,128)(2,1)S(1)}, u32[]{:S(2)}, u32[]{:S(2)}) collective-permute-start(bf16[256,512]{1,0:T(8,128)(2,1)S(1)} %fusion.26), channel_id=1, source_target_pairs={{0,8},{1,9},{2,10},{3,11},{4,12},{5,13},{6,14},{7,15},{8,0},{9,1},... | collective-permute-start | bytes 786440 | tf_op jit(solution)/shard_map/ppermute | solution.py:20
  259.2 12.1 %collective-permute-start.13 = (bf16[2,256,512]{2,1,0:T(8,128)(2,1)S(1)}, bf16[2,256,512]{2,1,0:T(8,128)(2,1)S(1)}, u32[]{:S(2)}, u32[]{:S(2)}) collective-permute-start(bf16[2,256,512]{2,1,0:T(8,128)(2,1)S(1)} %maximum_select_fusion), channel_id=1, source_target_pairs={{0,1},{1,2},{2,3},{3,4},{4,5},{5,6},{6,7},{7,0},{8,9},{9,10},{10,1... | collective-permute-start | bytes 1572872 | tf_op jit(solution)/shard_map/ppermute | solution.py:20
  264.0 13.0 %collective-permute-start.10 = (bf16[2,256,512]{2,1,0:T(8,128)(2,1)S(1)}, bf16[2,256,512]{2,1,0:T(8,128)(2,1)S(1)}, u32[]{:S(2)}, u32[]{:S(2)}) collective-permute-start(bf16[2,256,512]{2,1,0:T(8,128)(2,1)S(1)} %maximum_select_fusion), channel_id=1, source_target_pairs={{0,7},{1,0},{2,1},{3,2},{4,3},{5,4},{6,5},{7,6},{8,15},{9,8},{10,9... | collective-permute-start | bytes 1572872 | tf_op jit(solution)/shard_map/ppermute | solution.py:20
  271.3 12.6 %collective-permute-start.14 = (bf16[2,256,512]{2,1,0:T(8,128)(2,1)S(1)}, bf16[2,256,512]{2,1,0:T(8,128)(2,1)S(1)}, u32[]{:S(2)}, u32[]{:S(2)}) collective-permute-start(bf16[2,256,512]{2,1,0:T(8,128)(2,1)S(1)} %collective-permute-done.13), channel_id=1, source_target_pairs={{0,1},{1,2},{2,3},{3,4},{4,5},{5,6},{6,7},{7,0},{8,9},{9,10},{10,1... | collective-permute-start | bytes 1572872 | tf_op jit(solution)/shard_map/ppermute | solution.py:20
  276.9 12.7 %collective-permute-start.11 = (bf16[2,256,512]{2,1,0:T(8,128)(2,1)S(1)}, bf16[2,256,512]{2,1,0:T(8,128)(2,1)}, u32[]{:S(2)}, u32[]{:S(2)}) collective-permute-start(bf16[2,256,512]{2,1,0:T(8,128)(2,1)S(1)} %collective-permute-done.10), channel_id=1, source_target_pairs={{0,7},{1,0},{2,1},{3,2},{4,3},{5,4},{6,5},{7,6},{8,15},{9,8},{10,9... | collective-permute-start | bytes 1572872 | tf_op jit(solution)/shard_map/ppermute | solution.py:20
  283.9 13.7 %collective-permute-start.15 = (bf16[2,256,512]{2,1,0:T(8,128)(2,1)S(1)}, bf16[2,256,512]{2,1,0:T(8,128)(2,1)S(1)}, u32[]{:S(2)}, u32[]{:S(2)}) collective-permute-start(bf16[2,256,512]{2,1,0:T(8,128)(2,1)S(1)} %collective-permute-done.14), channel_id=1, source_target_pairs={{0,1},{1,2},{2,3},{3,4},{4,5},{5,6},{6,7},{7,0},{8,9},{9,10},{10,1... | collective-permute-start | bytes 1572872 | tf_op jit(solution)/shard_map/ppermute | solution.py:20
  289.7 23.7 %collective-permute-start.12 = (bf16[2,256,512]{2,1,0:T(8,128)(2,1)}, bf16[2,256,512]{2,1,0:T(8,128)(2,1)}, u32[]{:S(2)}, u32[]{:S(2)}) collective-permute-start(bf16[2,256,512]{2,1,0:T(8,128)(2,1)} %collective-permute-done.11), channel_id=1, source_target_pairs={{0,7},{1,0},{2,1},{3,2},{4,3},{5,4},{6,5},{7,6},{8,15},{9,8},{10,9... | collective-permute-start | bytes 1572872 | tf_op jit(solution)/shard_map/ppermute | solution.py:20
  297.6 17.6 %collective-permute-start.16 = (bf16[2,256,512]{2,1,0:T(8,128)(2,1)S(1)}, bf16[2,256,512]{2,1,0:T(8,128)(2,1)S(1)}, u32[]{:S(2)}, u32[]{:S(2)}) collective-permute-start(bf16[2,256,512]{2,1,0:T(8,128)(2,1)S(1)} %collective-permute-done.15), channel_id=1, source_target_pairs={{0,1},{1,2},{2,3},{3,4},{4,5},{5,6},{6,7},{7,0},{8,9},{9,10},{10,1... | collective-permute-start | bytes 1572872 | tf_op jit(solution)/shard_map/ppermute | solution.py:20

commit v5 on v0

--- a/solution.py
+++ b/solution.py
@@ -25,23 +25,48 @@
     ring = min(ring, size)
     halves = size // ring
     place = lax.axis_index(axis)
-    if halves == 2:
-        partner = shifted(block, axis, [(i, i ^ ring) for i in range(size)])
-        first = place // ring == 0
-        chunk = jnp.where(first, jnp.stack([block, partner]), jnp.stack([partner, block]))
-    else:
-        chunk = block[None]
     forward = [(i, (i // ring) * ring + (i % ring + 1) % ring) for i in range(size)]
     backward = [(i, (i // ring) * ring + (i % ring - 1) % ring) for i in range(size)]
-    ahead, behind = [], []
-    up, down = chunk, chunk
-    for step in range(ring // 2):
-        up = shifted(up, axis, forward)
-        behind.append(up)
-        if step < (ring - 1) // 2:
-            down = shifted(down, axis, backward)
-            ahead.append(down)
-    return [chunk] + ahead + behind[::-1]
+    up_steps, down_steps = ring // 2, (ring - 1) // 2
+    if halves != 2:
+        ahead, behind = [], []
+        up, down = block, block
+        for step in range(up_steps):
+            up = shifted(up, axis, forward)
+            behind.append(up)
+            if step < down_steps:
+                down = shifted(down, axis, backward)
+                ahead.append(down)
+        return [c[None] for c in [block] + ahead + behind[::-1]]
+    partner = shifted(block, axis, [(i, i ^ ring) for i in range(size)])
+    own_up, own_down, far_up, far_down = [], [], [], []
+    cur = {"ou": block, "od": block, "fu": partner, "fd": partner}
+    for rnd in range(up_steps + 1):
+        up_parts, down_parts = [], []
+        if rnd < up_steps:
+            up_parts.append("ou")
+        if rnd < down_steps:
+            down_parts.append("od")
+        if 1 <= rnd <= up_steps:
+            up_parts.append("fu")
+        if 1 <= rnd <= down_steps:
+            down_parts.append("fd")
+        for parts, route in ((up_parts, forward), (down_parts, backward)):
+            if not parts:
+                continue
+            moved = shifted(jnp.stack([cur[p] for p in parts]), axis, route)
+            for n, p in enumerate(parts):
+                cur[p] = moved[n]
+                {"ou": own_up, "od": own_down, "fu": far_up, "fd": far_down}[p].append(moved[n])
+    first = place // ring == 0
+
+    def pair(own, far):
+        return jnp.where(first, jnp.stack([own, far]), jnp.stack([far, own]))
+
+    chunks = [pair(block, partner)]
+    chunks += [pair(o, f) for o, f in zip(own_down, far_down)]
+    chunks += [pair(o, f) for o, f in zip(own_up, far_up)][::-1]
+    return chunks
 
 
 def entering_state(local_state, rate, tokens_here, axis):
@@ -109,11 +134,11 @@
     halves = features[0].shape[0]
     weight_all = weight_all.reshape(halves, ring, channels, weight_all.shape[1])
     place = lax.axis_index("tensor") % ring
+    weight_all = jnp.roll(weight_all, -place, axis=1)
     projected = jnp.zeros((features[0].shape[1], weight_all.shape[-1]), jnp.float32)
     for r in range(ring):
-        taken = lax.dynamic_index_in_dim(weight_all, (place + r) % ring, 1, False)
         projected = projected + jnp.einsum(
-            "htc,hco->to", features[r], taken, preferred_element_type=jnp.float32
+            "htc,hco->to", features[r], weight_all[:, r], preferred_element_type=jnp.float32
         )
     return projected.astype(jnp.bfloat16)
 

time: 151 us -> 155 us (1.026)
  the two profiles are of different devices: /device:TPU:26 before, /device:TPU:24 now
where the time goes in v5:
time: 155 us; the launch traced here: 154 us
  starting transfers between devices  79 us (51%)
  waiting for transfers between devices  30.9 us (20%)
  between operations  13.9 us (9%)
  other arithmetic  13.3 us (9%)
  matrix products  12.8 us (8%)
  local copies, waits for them, and re-layouts  4.27 us (3%)
    ppermute x9, starting transfers between devices, passed_along(): return lax.ppermute(block, axis, route)  42.4 us
    ppermute x10, starting transfers between devices, shifted(): return lax.ppermute(block, axis, route)  36.6 us
    ppermute x10, waiting for transfers between devices, shifted(): return lax.ppermute(block, axis, route)  26.8 us
    dot_general x1, matrix products, finish(): jnp.dot(lower, scaled, precision=PRECISE)  6.55 us
    dot_general x8, matrix products, finish(): jnp.einsum('htc,hco->to', features[r], weight_all[:, r], preferred_elemen...  6.25 us
    concatenate x1, other arithmetic, finish(): weight_all = jnp.roll(weight_all, -place, axis=1)  5.68 us
    ppermute x9, waiting for transfers between devices, passed_along(): return lax.ppermute(block, axis, route)  3.38 us
  transfers between devices with their start and end apart: 20, of which 8 were waited for; matrix products, arithmetic and copies ran while one was open for 17% of the time, Pallas kernels for 0%

profile of v5, /device:TPU:24, one launch (start us, length us, event | category | flops | bytes accessed | tf_op | source)
XLA Modules:
  0.0 154.3 jit_solution(17746167908403799136)
XLA Ops:
  14.9 7.6 %collective-permute-start.4 = (f32[16,512]{1,0:T(8,128)S(1)}, f32[16,512]{1,0:T(8,128)S(1)}, u32[]{:S(2)}, u32[]{:S(2)}) collective-permute-start(f32[16,512]{1,0:T(8,128)S(1)} %multiply_reduce_fusion.1), channel_id=1, source_target_pairs={{0,64},{16,80},{32,96},{48,112},{64,128},{80,144},{96,160},{112,17... | collective-permute-start | bytes 98312 | tf_op jit(solution)/shard_map/ppermute | solution.py:16
  22.5 5.9 %collective-permute-start.3 = (f32[16,512]{1,0:T(8,128)S(1)}, f32[16,512]{1,0:T(8,128)S(1)}, u32[]{:S(2)}, u32[]{:S(2)}) collective-permute-start(f32[16,512]{1,0:T(8,128)S(1)} %multiply_reduce_fusion.1), channel_id=1, source_target_pairs={{0,48},{16,64},{32,80},{48,96},{64,112},{80,128},{96,144},{112,160... | collective-permute-start | bytes 98312 | tf_op jit(solution)/shard_map/ppermute | solution.py:16
  28.4 3.4 %collective-permute-start.2 = (f32[16,512]{1,0:T(8,128)S(1)}, f32[16,512]{1,0:T(8,128)S(1)}, u32[]{:S(2)}, u32[]{:S(2)}) collective-permute-start(f32[16,512]{1,0:T(8,128)S(1)} %multiply_reduce_fusion.1), channel_id=1, source_target_pairs={{0,32},{16,48},{32,64},{48,80},{64,96},{80,112},{96,128},{112,144}... | collective-permute-start | bytes 98312 | tf_op jit(solution)/shard_map/ppermute | solution.py:16
  31.8 3.1 %collective-permute-start.1 = (f32[16,512]{1,0:T(8,128)S(1)}, f32[16,512]{1,0:T(8,128)S(1)}, u32[]{:S(2)}, u32[]{:S(2)}) collective-permute-start(f32[16,512]{1,0:T(8,128)S(1)} %multiply_reduce_fusion.1), channel_id=1, source_target_pairs={{0,16},{16,32},{32,48},{48,64},{64,80},{80,96},{96,112},{112,128},... | collective-permute-start | bytes 98312 | tf_op jit(solution)/shard_map/ppermute | solution.py:16
  35.8 6.0 %collective-permute-start.7 = (f32[16,512]{1,0:T(8,128)S(1)}, f32[16,512]{1,0:T(8,128)S(1)}, u32[]{:S(2)}, u32[]{:S(2)}) collective-permute-start(f32[16,512]{1,0:T(8,128)S(1)} %multiply_add_fusion.1), channel_id=1, source_target_pairs={{0,192},{16,208},{32,224},{48,240},{64,256},{80,272},{96,288},{112... | collective-permute-start | bytes 98312 | tf_op jit(solution)/shard_map/ppermute | solution.py:16
  41.8 6.8 %collective-permute-start.6 = (f32[16,512]{1,0:T(8,128)S(1)}, f32[16,512]{1,0:T(8,128)S(1)}, u32[]{:S(2)}, u32[]{:S(2)}) collective-permute-start(f32[16,512]{1,0:T(8,128)S(1)} %multiply_add_fusion.1), channel_id=1, source_target_pairs={{0,128},{16,144},{32,160},{48,176},{64,192},{80,208},{96,224},{112... | collective-permute-start | bytes 98312 | tf_op jit(solution)/shard_map/ppermute | solution.py:16
  48.6 3.1 %collective-permute-start.5 = (f32[16,512]{1,0:T(8,128)S(1)}, f32[16,512]{1,0:T(8,128)S(1)}, u32[]{:S(2)}, u32[]{:S(2)}) collective-permute-start(f32[16,512]{1,0:T(8,128)S(1)} %multiply_add_fusion.1), channel_id=1, source_target_pairs={{0,64},{16,80},{32,96},{48,112},{64,128},{80,144},{96,160},{112,17... | collective-permute-start | bytes 98312 | tf_op jit(solution)/shard_map/ppermute | solution.py:16
  51.8 2.2 %collective-permute-done.5 = f32[16,512]{1,0:T(8,128)S(1)} collective-permute-done((f32[16,512]{1,0:T(8,128)S(1)}, f32[16,512]{1,0:T(8,128)S(1)}, u32[]{:S(2)}, u32[]{:S(2)}) %collective-permute-start.5) | collective-permute-done | bytes 32800 | tf_op jit(solution)/shard_map/ppermute | solution.py:16
  54.0 4.7 %collective-permute-start.8 = (f32[16,512]{1,0:T(8,128)S(1)}, f32[16,512]{1,0:T(8,128)S(1)}, u32[]{:S(2)}, u32[]{:S(2)}) collective-permute-start(f32[16,512]{1,0:T(8,128)S(1)} %multiply_add_fusion), channel_id=1, source_target_pairs={{0,256},{16,272},{32,288},{48,304},{64,320},{80,336},{96,352},{112... | collective-permute-start | bytes 98312 | tf_op jit(solution)/shard_map/ppermute | solution.py:16
  62.1 6.6 %multiply_reduce_fusion.2 = f32[256,512]{1,0:T(8,128)S(1)} fusion(f32[16,512]{1,0:T(8,128)S(1)} %neg.8, f32[16,512]{1,0:T(8,128)S(1)} %get-tuple-element.6, f32[16,512,256]{2,1,0:T(8,128)S(1)} %bitcast.107), kind=kOutput, calls=%fused_computation.6 | convolution fusion | flops 6450774016 | bytes 8978432 | tf_op jit(solution)/shard_map/dot_general | solution.py:122
  69.3 4.5 %collective-permute-start.14 = (bf16[1,256,512]{2,1,0:T(8,128)(2,1)S(1)}, bf16[1,256,512]{2,1,0:T(8,128)(2,1)S(1)}, u32[]{:S(2)}, u32[]{:S(2)}) collective-permute-start(bf16[1,256,512]{2,1,0:T(8,128)(2,1)S(1)} %fusion.56), channel_id=1, source_target_pairs={{0,1},{1,2},{2,3},{3,4},{4,5},{5,6},{6,7},{7,0},{8,9},{9,10},{10,1... | collective-permute-start | bytes 786440 | tf_op jit(solution)/shard_map/ppermute | solution.py:20
  73.8 4.5 %collective-permute-start.9 = (bf16[256,512]{1,0:T(8,128)(2,1)S(1)}, bf16[256,512]{1,0:T(8,128)(2,1)S(1)}, u32[]{:S(2)}, u32[]{:S(2)}) collective-permute-start(bf16[256,512]{1,0:T(8,128)(2,1)S(1)} %fusion.54), channel_id=1, source_target_pairs={{0,8},{1,9},{2,10},{3,11},{4,12},{5,13},{6,14},{7,15},{8,0},{9,1},... | collective-permute-start | bytes 786440 | tf_op jit(solution)/shard_map/ppermute | solution.py:20
  78.4 1.9 %collective-permute-start.10 = (bf16[1,256,512]{2,1,0:T(8,128)(2,1)S(1)}, bf16[1,256,512]{2,1,0:T(8,128)(2,1)S(1)}, u32[]{:S(2)}, u32[]{:S(2)}) collective-permute-start(bf16[1,256,512]{2,1,0:T(8,128)(2,1)S(1)} %fusion.56), channel_id=1, source_target_pairs={{0,7},{1,0},{2,1},{3,2},{4,3},{5,4},{6,5},{7,6},{8,15},{9,8},{10,9... | collective-permute-start | bytes 786440 | tf_op jit(solution)/shard_map/ppermute | solution.py:20
  80.3 8.8 %collective-permute-done.9 = bf16[256,512]{1,0:T(8,128)(2,1)S(1)} collective-permute-done((bf16[256,512]{1,0:T(8,128)(2,1)S(1)}, bf16[256,512]{1,0:T(8,128)(2,1)S(1)}, u32[]{:S(2)}, u32[]{:S(2)}) %collective-permute-start.9) | collective-permute-done | bytes 262176 | tf_op jit(solution)/shard_map/ppermute | solution.py:20
  89.2 3.8 %collective-permute-start.15 = (bf16[2,256,512]{2,1,0:T(8,128)(2,1)S(1)}, bf16[2,256,512]{2,1,0:T(8,128)(2,1)S(1)}, u32[]{:S(2)}, u32[]{:S(2)}) collective-permute-start(bf16[2,256,512]{2,1,0:T(8,128)(2,1)S(1)} %get-tuple-element.18), channel_id=1, source_target_pairs={{0,1},{1,2},{2,3},{3,4},{4,5},{5,6},{6,7},{7,0},{8,9},{9,10},{10,1... | collective-permute-start | bytes 1572872 | tf_op jit(solution)/shard_map/ppermute | solution.py:20
  93.0 2.1 %collective-permute-start.11 = (bf16[2,256,512]{2,1,0:T(8,128)(2,1)S(1)}, bf16[2,256,512]{2,1,0:T(8,128)(2,1)S(1)}, u32[]{:S(2)}, u32[]{:S(2)}) collective-permute-start(bf16[2,256,512]{2,1,0:T(8,128)(2,1)S(1)} %get-tuple-element.17), channel_id=1, source_target_pairs={{0,7},{1,0},{2,1},{3,2},{4,3},{5,4},{6,5},{7,6},{8,15},{9,8},{10,9... | collective-permute-start | bytes 1572872 | tf_op jit(solution)/shard_map/ppermute | solution.py:20
  95.1 6.2 %collective-permute-done.15 = bf16[2,256,512]{2,1,0:T(8,128)(2,1)S(1)} collective-permute-done((bf16[2,256,512]{2,1,0:T(8,128)(2,1)S(1)}, bf16[2,256,512]{2,1,0:T(8,128)(2,1)S(1)}, u32[]{:S(2)}, u32[]{:S(2)}) %collective-permute-start.15) | collective-permute-done | bytes 524320 | tf_op jit(solution)/shard_map/ppermute | solution.py:20
  101.3 4.6 %collective-permute-start.16 = (bf16[2,256,512]{2,1,0:T(8,128)(2,1)S(1)}, bf16[2,256,512]{2,1,0:T(8,128)(2,1)S(1)}, u32[]{:S(2)}, u32[]{:S(2)}) collective-permute-start(bf16[2,256,512]{2,1,0:T(8,128)(2,1)S(1)} %collective-permute-done.15), channel_id=1, source_target_pairs={{0,1},{1,2},{2,3},{3,4},{4,5},{5,6},{6,7},{7,0},{8,9},{9,10},{10,1... | collective-permute-start | bytes 1572872 | tf_op jit(solution)/shard_map/ppermute | solution.py:20
  108.9 5.5 %collective-permute-done.16 = bf16[2,256,512]{2,1,0:T(8,128)(2,1)S(1)} collective-permute-done((bf16[2,256,512]{2,1,0:T(8,128)(2,1)S(1)}, bf16[2,256,512]{2,1,0:T(8,128)(2,1)S(1)}, u32[]{:S(2)}, u32[]{:S(2)}) %collective-permute-start.16) | collective-permute-done | bytes 524320 | tf_op jit(solution)/shard_map/ppermute | solution.py:20
  114.4 5.6 %collective-permute-start.17 = (bf16[2,256,512]{2,1,0:T(8,128)(2,1)S(1)}, bf16[2,256,512]{2,1,0:T(8,128)(2,1)S(1)}, u32[]{:S(2)}, u32[]{:S(2)}) collective-permute-start(bf16[2,256,512]{2,1,0:T(8,128)(2,1)S(1)} %collective-permute-done.16), channel_id=1, source_target_pairs={{0,1},{1,2},{2,3},{3,4},{4,5},{5,6},{6,7},{7,0},{8,9},{9,10},{10,1... | collective-permute-start | bytes 1572872 | tf_op jit(solution)/shard_map/ppermute | solution.py:20
  121.6 1.9 %collective-permute-start.13 = (bf16[1,256,512]{2,1,0:T(8,128)(2,1)S(1)}, bf16[1,256,512]{2,1,0:T(8,128)(2,1)}, u32[]{:S(2)}, u32[]{:S(2)}) collective-permute-start(bf16[1,256,512]{2,1,0:T(8,128)(2,1)S(1)} %get-tuple-element.12), channel_id=1, source_target_pairs={{0,7},{1,0},{2,1},{3,2},{4,3},{5,4},{6,5},{7,6},{8,15},{9,8},{10,9... | collective-permute-start | bytes 786440 | tf_op jit(solution)/shard_map/ppermute | solution.py:20
  123.5 5.9 %collective-permute-done.17 = bf16[2,256,512]{2,1,0:T(8,128)(2,1)S(1)} collective-permute-done((bf16[2,256,512]{2,1,0:T(8,128)(2,1)S(1)}, bf16[2,256,512]{2,1,0:T(8,128)(2,1)S(1)}, u32[]{:S(2)}, u32[]{:S(2)}) %collective-permute-start.17) | collective-permute-done | bytes 524320 | tf_op jit(solution)/shard_map/ppermute | solution.py:20
  129.5 5.8 %collective-permute-start.18 = (bf16[1,256,512]{2,1,0:T(8,128)(2,1)S(1)}, bf16[1,256,512]{2,1,0:T(8,128)(2,1)}, u32[]{:S(2)}, u32[]{:S(2)}) collective-permute-start(bf16[1,256,512]{2,1,0:T(8,128)(2,1)S(1)} %get-tuple-element.14), channel_id=1, source_target_pairs={{0,1},{1,2},{2,3},{3,4},{4,5},{5,6},{6,7},{7,0},{8,9},{9,10},{10,1... | collective-permute-start | bytes 786440 | tf_op jit(solution)/shard_map/ppermute | solution.py:20
  135.4 5.7 %fusion = bf16[2,8,512,512]{3,2,1,0:T(8,128)(2,1)S(1)} fusion(s32[]{:T(128)S(6)} %select_n.64, bf16[2,8,512,512]{3,2,1,0:T(8,128)(2,1)} %bitcast.106), kind=kLoop, calls=%fused_computation.2 | loop fusion | flops 4194304 | bytes 16777220 | tf_op jit(solution)/shard_map/jit(_roll_dynamic)/concatenate | solution.py:137
  (67 shorter events, 24.0 us)
Async XLA Ops:
  6.5 29.2 %copy-start = (f32[16,512]{1,0:T(8,128)S(1)}, f32[16,512]{1,0:T(8,128)}, u32[]{:S(2)}) copy-start(f32[16,512]{1,0:T(8,128)} %param.8) | copy-start | bytes 98308
  6.5 128.8 %all-gather.2.cloned.1.call-start = ((), (), s32[]{:S(2)}) async-start(), calls=%async_computation | async-start | bytes 8650752 | tf_op jit(solution)/shard_map/all_gather | solution.py:132
  8.0 3.4 %collective-permute-start = (bf16[3,2,512]{2,1,0:T(2,128)(2,1)S(1)}, bf16[3,2,512]{2,1,0:T(2,128)(2,1)S(1)}, u32[]{:S(2)}, u32[]{:S(2)}) collective-permute-start(bf16[3,2,512]{2,1,0:T(2,128)(2,1)S(1)} %slice.96), channel_id=1, source_target_pairs={{0,16},{16,32},{32,48},{48,64},{64,80},{80,96},{96,112},{112,128},... | collective-permute-start | bytes 18440 | tf_op jit(solution)/shard_map/ppermute | solution.py:16
  13.3 47.3 %copy-start.5 = (f32[16,512]{1,0:T(8,128)S(1)}, f32[16,512]{1,0:T(8,128)}, u32[]{:S(2)}) copy-start(f32[16,512]{1,0:T(8,128)} %param.9) | copy-start | bytes 98308
  14.9 20.1 %collective-permute-start.4 = (f32[16,512]{1,0:T(8,128)S(1)}, f32[16,512]{1,0:T(8,128)S(1)}, u32[]{:S(2)}, u32[]{:S(2)}) collective-permute-start(f32[16,512]{1,0:T(8,128)S(1)} %multiply_reduce_fusion.1), channel_id=1, source_target_pairs={{0,64},{16,80},{32,96},{48,112},{64,128},{80,144},{96,160},{112,17... | collective-permute-start | bytes 98312 | tf_op jit(solution)/shard_map/ppermute | solution.py:16
  22.5 12.5 %collective-permute-start.3 = (f32[16,512]{1,0:T(8,128)S(1)}, f32[16,512]{1,0:T(8,128)S(1)}, u32[]{:S(2)}, u32[]{:S(2)}) collective-permute-start(f32[16,512]{1,0:T(8,128)S(1)} %multiply_reduce_fusion.1), channel_id=1, source_target_pairs={{0,48},{16,64},{32,80},{48,96},{64,112},{80,128},{96,144},{112,160... | collective-permute-start | bytes 98312 | tf_op jit(solution)/shard_map/ppermute | solution.py:16
  28.4 6.5 %collective-permute-start.2 = (f32[16,512]{1,0:T(8,128)S(1)}, f32[16,512]{1,0:T(8,128)S(1)}, u32[]{:S(2)}, u32[]{:S(2)}) collective-permute-start(f32[16,512]{1,0:T(8,128)S(1)} %multiply_reduce_fusion.1), channel_id=1, source_target_pairs={{0,32},{16,48},{32,64},{48,80},{64,96},{80,112},{96,128},{112,144}... | collective-permute-start | bytes 98312 | tf_op jit(solution)/shard_map/ppermute | solution.py:16
  31.8 3.9 %collective-permute-start.1 = (f32[16,512]{1,0:T(8,128)S(1)}, f32[16,512]{1,0:T(8,128)S(1)}, u32[]{:S(2)}, u32[]{:S(2)}) collective-permute-start(f32[16,512]{1,0:T(8,128)S(1)} %multiply_reduce_fusion.1), channel_id=1, source_target_pairs={{0,16},{16,32},{32,48},{48,64},{64,80},{80,96},{96,112},{112,128},... | collective-permute-start | bytes 98312 | tf_op jit(solution)/shard_map/ppermute | solution.py:16
  35.8 16.0 %collective-permute-start.7 = (f32[16,512]{1,0:T(8,128)S(1)}, f32[16,512]{1,0:T(8,128)S(1)}, u32[]{:S(2)}, u32[]{:S(2)}) collective-permute-start(f32[16,512]{1,0:T(8,128)S(1)} %multiply_add_fusion.1), channel_id=1, source_target_pairs={{0,192},{16,208},{32,224},{48,240},{64,256},{80,272},{96,288},{112... | collective-permute-start | bytes 98312 | tf_op jit(solution)/shard_map/ppermute | solution.py:16
  41.8 10.0 %collective-permute-start.6 = (f32[16,512]{1,0:T(8,128)S(1)}, f32[16,512]{1,0:T(8,128)S(1)}, u32[]{:S(2)}, u32[]{:S(2)}) collective-permute-start(f32[16,512]{1,0:T(8,128)S(1)} %multiply_add_fusion.1), channel_id=1, source_target_pairs={{0,128},{16,144},{32,160},{48,176},{64,192},{80,208},{96,224},{112... | collective-permute-start | bytes 98312 | tf_op jit(solution)/shard_map/ppermute | solution.py:16
  48.6 5.4 %collective-permute-start.5 = (f32[16,512]{1,0:T(8,128)S(1)}, f32[16,512]{1,0:T(8,128)S(1)}, u32[]{:S(2)}, u32[]{:S(2)}) collective-permute-start(f32[16,512]{1,0:T(8,128)S(1)} %multiply_add_fusion.1), channel_id=1, source_target_pairs={{0,64},{16,80},{32,96},{48,112},{64,128},{80,144},{96,160},{112,17... | collective-permute-start | bytes 98312 | tf_op jit(solution)/shard_map/ppermute | solution.py:16
  54.0 6.5 %collective-permute-start.8 = (f32[16,512]{1,0:T(8,128)S(1)}, f32[16,512]{1,0:T(8,128)S(1)}, u32[]{:S(2)}, u32[]{:S(2)}) collective-permute-start(f32[16,512]{1,0:T(8,128)S(1)} %multiply_add_fusion), channel_id=1, source_target_pairs={{0,256},{16,272},{32,288},{48,304},{64,320},{80,336},{96,352},{112... | collective-permute-start | bytes 98312 | tf_op jit(solution)/shard_map/ppermute | solution.py:16
  60.2 8.4 %copy-start.6 = (f32[512]{0:T(512)S(1)}, f32[512]{0:T(512)}, u32[]{:S(2)}) copy-start(f32[512]{0:T(512)} %param.10) | copy-start | bytes 6148
  69.3 11.0 %collective-permute-start.14 = (bf16[1,256,512]{2,1,0:T(8,128)(2,1)S(1)}, bf16[1,256,512]{2,1,0:T(8,128)(2,1)S(1)}, u32[]{:S(2)}, u32[]{:S(2)}) collective-permute-start(bf16[1,256,512]{2,1,0:T(8,128)(2,1)S(1)} %fusion.56), channel_id=1, source_target_pairs={{0,1},{1,2},{2,3},{3,4},{4,5},{5,6},{6,7},{7,0},{8,9},{9,10},{10,1... | collective-permute-start | bytes 786440 | tf_op jit(solution)/shard_map/ppermute | solution.py:20
  73.8 15.3 %collective-permute-start.9 = (bf16[256,512]{1,0:T(8,128)(2,1)S(1)}, bf16[256,512]{1,0:T(8,128)(2,1)S(1)}, u32[]{:S(2)}, u32[]{:S(2)}) collective-permute-start(bf16[256,512]{1,0:T(8,128)(2,1)S(1)} %fusion.54), channel_id=1, source_target_pairs={{0,8},{1,9},{2,10},{3,11},{4,12},{5,13},{6,14},{7,15},{8,0},{9,1},... | collective-permute-start | bytes 786440 | tf_op jit(solution)/shard_map/ppermute | solution.py:20
  78.4 10.8 %collective-permute-start.10 = (bf16[1,256,512]{2,1,0:T(8,128)(2,1)S(1)}, bf16[1,256,512]{2,1,0:T(8,128)(2,1)S(1)}, u32[]{:S(2)}, u32[]{:S(2)}) collective-permute-start(bf16[1,256,512]{2,1,0:T(8,128)(2,1)S(1)} %fusion.56), channel_id=1, source_target_pairs={{0,7},{1,0},{2,1},{3,2},{4,3},{5,4},{6,5},{7,6},{8,15},{9,8},{10,9... | collective-permute-start | bytes 786440 | tf_op jit(solution)/shard_map/ppermute | solution.py:20
  89.2 12.1 %collective-permute-start.15 = (bf16[2,256,512]{2,1,0:T(8,128)(2,1)S(1)}, bf16[2,256,512]{2,1,0:T(8,128)(2,1)S(1)}, u32[]{:S(2)}, u32[]{:S(2)}) collective-permute-start(bf16[2,256,512]{2,1,0:T(8,128)(2,1)S(1)} %get-tuple-element.18), channel_id=1, source_target_pairs={{0,1},{1,2},{2,3},{3,4},{4,5},{5,6},{6,7},{7,0},{8,9},{9,10},{10,1... | collective-permute-start | bytes 1572872 | tf_op jit(solution)/shard_map/ppermute | solution.py:20
  93.0 13.2 %collective-permute-start.11 = (bf16[2,256,512]{2,1,0:T(8,128)(2,1)S(1)}, bf16[2,256,512]{2,1,0:T(8,128)(2,1)S(1)}, u32[]{:S(2)}, u32[]{:S(2)}) collective-permute-start(bf16[2,256,512]{2,1,0:T(8,128)(2,1)S(1)} %get-tuple-element.17), channel_id=1, source_target_pairs={{0,7},{1,0},{2,1},{3,2},{4,3},{5,4},{6,5},{7,6},{8,15},{9,8},{10,9... | collective-permute-start | bytes 1572872 | tf_op jit(solution)/shard_map/ppermute | solution.py:20
  101.3 13.1 %collective-permute-start.16 = (bf16[2,256,512]{2,1,0:T(8,128)(2,1)S(1)}, bf16[2,256,512]{2,1,0:T(8,128)(2,1)S(1)}, u32[]{:S(2)}, u32[]{:S(2)}) collective-permute-start(bf16[2,256,512]{2,1,0:T(8,128)(2,1)S(1)} %collective-permute-done.15), channel_id=1, source_target_pairs={{0,1},{1,2},{2,3},{3,4},{4,5},{5,6},{6,7},{7,0},{8,9},{9,10},{10,1... | collective-permute-start | bytes 1572872 | tf_op jit(solution)/shard_map/ppermute | solution.py:20
  106.2 14.6 %collective-permute-start.12 = (bf16[2,256,512]{2,1,0:T(8,128)(2,1)S(1)}, bf16[2,256,512]{2,1,0:T(8,128)(2,1)S(1)}, u32[]{:S(2)}, u32[]{:S(2)}) collective-permute-start(bf16[2,256,512]{2,1,0:T(8,128)(2,1)S(1)} %collective-permute-done.11), channel_id=1, source_target_pairs={{0,7},{1,0},{2,1},{3,2},{4,3},{5,4},{6,5},{7,6},{8,15},{9,8},{10,9... | collective-permute-start | bytes 1572872 | tf_op jit(solution)/shard_map/ppermute | solution.py:20
  114.4 15.1 %collective-permute-start.17 = (bf16[2,256,512]{2,1,0:T(8,128)(2,1)S(1)}, bf16[2,256,512]{2,1,0:T(8,128)(2,1)S(1)}, u32[]{:S(2)}, u32[]{:S(2)}) collective-permute-start(bf16[2,256,512]{2,1,0:T(8,128)(2,1)S(1)} %collective-permute-done.16), channel_id=1, source_target_pairs={{0,1},{1,2},{2,3},{3,4},{4,5},{5,6},{6,7},{7,0},{8,9},{9,10},{10,1... | collective-permute-start | bytes 1572872 | tf_op jit(solution)/shard_map/ppermute | solution.py:20
  121.6 22.3 %collective-permute-start.13 = (bf16[1,256,512]{2,1,0:T(8,128)(2,1)S(1)}, bf16[1,256,512]{2,1,0:T(8,128)(2,1)}, u32[]{:S(2)}, u32[]{:S(2)}) collective-permute-start(bf16[1,256,512]{2,1,0:T(8,128)(2,1)S(1)} %get-tuple-element.12), channel_id=1, source_target_pairs={{0,7},{1,0},{2,1},{3,2},{4,3},{5,4},{6,5},{7,6},{8,15},{9,8},{10,9... | collective-permute-start | bytes 786440 | tf_op jit(solution)/shard_map/ppermute | solution.py:20
  129.5 12.4 %collective-permute-start.18 = (bf16[1,256,512]{2,1,0:T(8,128)(2,1)S(1)}, bf16[1,256,512]{2,1,0:T(8,128)(2,1)}, u32[]{:S(2)}, u32[]{:S(2)}) collective-permute-start(bf16[1,256,512]{2,1,0:T(8,128)(2,1)S(1)} %get-tuple-element.14), channel_id=1, source_target_pairs={{0,1},{1,2},{2,3},{3,4},{4,5},{5,6},{6,7},{7,0},{8,9},{9,10},{10,1... | collective-permute-start | bytes 786440 | tf_op jit(solution)/shard_map/ppermute | solution.py:20
  135.3 6.2 %copy-start.4 = (bf16[1,256,512]{2,1,0:T(8,128)(2,1)S(1)}, bf16[1,256,512]{2,1,0:T(8,128)(2,1)}, u32[]{:S(2)}) copy-start(bf16[1,256,512]{2,1,0:T(8,128)(2,1)} %get-tuple-element.10) | copy-start | bytes 786436
  (3 other events, 12.4 us)
Sparse Core Ops, SparseCore 0:
  9.5 82.8 all-gather.1

commit v6 on v0

--- a/solution.py
+++ b/solution.py
@@ -5,9 +5,6 @@
 
 
 KS = 3
-
-
-PRECISE = lax.Precision.HIGHEST
 
 
 def passed_along(block, axis, distance):
@@ -94,7 +91,7 @@
     growth = jnp.exp(rate[None] * lags)
     scaled = (growth * product[:, None, :]).reshape(tokens_here, modes * channels)
     lower = (jnp.arange(tokens_here)[:, None] >= jnp.arange(tokens_here)[None, :]).astype(jnp.float32)
-    running = jnp.dot(lower, scaled, precision=PRECISE).reshape(tokens_here, modes, channels)
+    running = jnp.dot(lower, scaled, precision=lax.Precision.HIGH).reshape(tokens_here, modes, channels)
     shrink = jnp.exp(-rate[None] * lags)
     inner = jnp.sum(mode_weight[None] * shrink * running, axis=1)
     carried = jnp.sum(
@@ -109,11 +106,11 @@
     halves = features[0].shape[0]
     weight_all = weight_all.reshape(halves, ring, channels, weight_all.shape[1])
     place = lax.axis_index("tensor") % ring
+    weight_all = jnp.roll(weight_all, -place, axis=1)
     projected = jnp.zeros((features[0].shape[1], weight_all.shape[-1]), jnp.float32)
     for r in range(ring):
-        taken = lax.dynamic_index_in_dim(weight_all, (place + r) % ring, 1, False)
         projected = projected + jnp.einsum(
-            "htc,hco->to", features[r], taken, preferred_element_type=jnp.float32
+            "htc,hco->to", features[r], weight_all[:, r], preferred_element_type=jnp.float32
         )
     return projected.astype(jnp.bfloat16)
 

time: 151 us -> 151 us (level)
  the two profiles are of different devices: /device:TPU:26 before, /device:TPU:30 now
where the time goes in v6:
time: 151 us; the launch traced here: 150 us
  starting transfers between devices  55.9 us (37%)
  waiting for transfers between devices  55.3 us (37%)
  between operations  13.9 us (9%)
  other arithmetic  13.3 us (9%)
  matrix products  9.61 us (6%)
  local copies, waits for them, and re-layouts  1.86 us (1%)
    ppermute x8, waiting for transfers between devices, shifted(): return lax.ppermute(block, axis, route)  31.3 us
    ppermute x8, starting transfers between devices, shifted(): return lax.ppermute(block, axis, route)  30.5 us
    ppermute x9, starting transfers between devices, passed_along(): return lax.ppermute(block, axis, route)  25.4 us
    ppermute x9, waiting for transfers between devices, passed_along(): return lax.ppermute(block, axis, route)  23.3 us
    concatenate x1, other arithmetic, finish(): weight_all = jnp.roll(weight_all, -place, axis=1)  5.68 us
    dot_general x8, matrix products, finish(): jnp.einsum('htc,hco->to', features[r], weight_all[:, r], preferred_elemen...  5.22 us
    dot_general x1, matrix products, finish(): jnp.dot(lower, scaled, precision=lax.Precision.HIGH)  4.38 us
  transfers between devices with their start and end apart: 18, of which 12 were waited for; matrix products, arithmetic and copies ran while one was open for 16% of the time, Pallas kernels for 0%

profile of v6, /device:TPU:30, one launch (start us, length us, event | category | flops | bytes accessed | tf_op | source)
XLA Modules:
  0.0 149.9 jit_solution(5348373876800282262)
XLA Ops:
  8.0 1.9 %collective-permute-start = (bf16[3,2,512]{2,1,0:T(2,128)(2,1)S(1)}, bf16[3,2,512]{2,1,0:T(2,128)(2,1)S(1)}, u32[]{:S(2)}, u32[]{:S(2)}) collective-permute-start(bf16[3,2,512]{2,1,0:T(2,128)(2,1)S(1)} %slice.55), channel_id=1, source_target_pairs={{0,16},{16,32},{32,48},{48,64},{64,80},{80,96},{96,112},{112,128},... | collective-permute-start | bytes 18440 | tf_op jit(solution)/shard_map/ppermute | solution.py:13
  11.6 8.4 %collective-permute-done = bf16[3,2,512]{2,1,0:T(2,128)(2,1)S(1)} collective-permute-done((bf16[3,2,512]{2,1,0:T(2,128)(2,1)S(1)}, bf16[3,2,512]{2,1,0:T(2,128)(2,1)S(1)}, u32[]{:S(2)}, u32[]{:S(2)}) %collective-permute-start) | collective-permute-done | bytes 6176 | tf_op jit(solution)/shard_map/ppermute | solution.py:13
  23.4 1.9 %collective-permute-start.1 = (f32[16,512]{1,0:T(8,128)S(1)}, f32[16,512]{1,0:T(8,128)S(1)}, u32[]{:S(2)}, u32[]{:S(2)}) collective-permute-start(f32[16,512]{1,0:T(8,128)S(1)} %multiply_reduce_fusion.1), channel_id=1, source_target_pairs={{0,16},{16,32},{32,48},{48,64},{64,80},{80,96},{96,112},{112,128},... | collective-permute-start | bytes 98312 | tf_op jit(solution)/shard_map/ppermute | solution.py:13
  25.3 1.9 %collective-permute-start.2 = (f32[16,512]{1,0:T(8,128)S(1)}, f32[16,512]{1,0:T(8,128)S(1)}, u32[]{:S(2)}, u32[]{:S(2)}) collective-permute-start(f32[16,512]{1,0:T(8,128)S(1)} %multiply_reduce_fusion.1), channel_id=1, source_target_pairs={{0,32},{16,48},{32,64},{48,80},{64,96},{80,112},{96,128},{112,144}... | collective-permute-start | bytes 98312 | tf_op jit(solution)/shard_map/ppermute | solution.py:13
  27.3 1.9 %collective-permute-start.3 = (f32[16,512]{1,0:T(8,128)S(1)}, f32[16,512]{1,0:T(8,128)S(1)}, u32[]{:S(2)}, u32[]{:S(2)}) collective-permute-start(f32[16,512]{1,0:T(8,128)S(1)} %multiply_reduce_fusion.1), channel_id=1, source_target_pairs={{0,48},{16,64},{32,80},{48,96},{64,112},{80,128},{96,144},{112,160... | collective-permute-start | bytes 98312 | tf_op jit(solution)/shard_map/ppermute | solution.py:13
  29.2 5.9 %collective-permute-start.4 = (f32[16,512]{1,0:T(8,128)S(1)}, f32[16,512]{1,0:T(8,128)S(1)}, u32[]{:S(2)}, u32[]{:S(2)}) collective-permute-start(f32[16,512]{1,0:T(8,128)S(1)} %multiply_reduce_fusion.1), channel_id=1, source_target_pairs={{0,64},{16,80},{32,96},{48,112},{64,128},{80,144},{96,160},{112,17... | collective-permute-start | bytes 98312 | tf_op jit(solution)/shard_map/ppermute | solution.py:13
  36.7 2.9 %collective-permute-done.4 = f32[16,512]{1,0:T(8,128)S(1)} collective-permute-done((f32[16,512]{1,0:T(8,128)S(1)}, f32[16,512]{1,0:T(8,128)S(1)}, u32[]{:S(2)}, u32[]{:S(2)}) %collective-permute-start.4) | collective-permute-done | bytes 32800 | tf_op jit(solution)/shard_map/ppermute | solution.py:13
  39.7 2.8 %collective-permute-start.5 = (f32[16,512]{1,0:T(8,128)S(1)}, f32[16,512]{1,0:T(8,128)S(1)}, u32[]{:S(2)}, u32[]{:S(2)}) collective-permute-start(f32[16,512]{1,0:T(8,128)S(1)} %multiply_add_fusion.1), channel_id=1, source_target_pairs={{0,64},{16,80},{32,96},{48,112},{64,128},{80,144},{96,160},{112,17... | collective-permute-start | bytes 98312 | tf_op jit(solution)/shard_map/ppermute | solution.py:13
  42.5 5.8 %collective-permute-start.6 = (f32[16,512]{1,0:T(8,128)S(1)}, f32[16,512]{1,0:T(8,128)S(1)}, u32[]{:S(2)}, u32[]{:S(2)}) collective-permute-start(f32[16,512]{1,0:T(8,128)S(1)} %multiply_add_fusion.1), channel_id=1, source_target_pairs={{0,128},{16,144},{32,160},{48,176},{64,192},{80,208},{96,224},{112... | collective-permute-start | bytes 98312 | tf_op jit(solution)/shard_map/ppermute | solution.py:13
  50.2 3.7 %collective-permute-done.6 = f32[16,512]{1,0:T(8,128)S(1)} collective-permute-done((f32[16,512]{1,0:T(8,128)S(1)}, f32[16,512]{1,0:T(8,128)S(1)}, u32[]{:S(2)}, u32[]{:S(2)}) %collective-permute-start.6) | collective-permute-done | bytes 32800 | tf_op jit(solution)/shard_map/ppermute | solution.py:13
  53.9 3.4 %collective-permute-done.7 = f32[16,512]{1,0:T(8,128)S(1)} collective-permute-done((f32[16,512]{1,0:T(8,128)S(1)}, f32[16,512]{1,0:T(8,128)S(1)}, u32[]{:S(2)}, u32[]{:S(2)}) %collective-permute-start.7) | collective-permute-done | bytes 32800 | tf_op jit(solution)/shard_map/ppermute | solution.py:13
  60.1 3.4 %collective-permute-done.8 = f32[16,512]{1,0:T(8,128)S(1)} collective-permute-done((f32[16,512]{1,0:T(8,128)S(1)}, f32[16,512]{1,0:T(8,128)S(1)}, u32[]{:S(2)}, u32[]{:S(2)}) %collective-permute-start.8) | collective-permute-done | bytes 32800 | tf_op jit(solution)/shard_map/ppermute | solution.py:13
  65.0 4.4 %multiply_reduce_fusion.2 = f32[256,512]{1,0:T(8,128)S(1)} fusion(f32[16,512]{1,0:T(8,128)S(1)} %neg.8, f32[16,512]{1,0:T(8,128)S(1)} %get-tuple-element.6, f32[16,512,256]{2,1,0:T(8,128)S(1)} %bitcast.115), kind=kOutput, calls=%fused_computation.6 | convolution fusion | flops 3229548544 | bytes 8978432 | tf_op jit(solution)/shard_map/dot_general | solution.py:94
  69.7 3.5 %collective-permute-start.9 = (bf16[256,512]{1,0:T(8,128)(2,1)S(1)}, bf16[256,512]{1,0:T(8,128)(2,1)S(1)}, u32[]{:S(2)}, u32[]{:S(2)}) collective-permute-start(bf16[256,512]{1,0:T(8,128)(2,1)S(1)} %fusion.11), channel_id=1, source_target_pairs={{0,8},{1,9},{2,10},{3,11},{4,12},{5,13},{6,14},{7,15},{8,0},{9,1},... | collective-permute-start | bytes 786440 | tf_op jit(solution)/shard_map/ppermute | solution.py:17
  73.6 12.6 %collective-permute-done.9 = bf16[256,512]{1,0:T(8,128)(2,1)S(1)} collective-permute-done((bf16[256,512]{1,0:T(8,128)(2,1)S(1)}, bf16[256,512]{1,0:T(8,128)(2,1)S(1)}, u32[]{:S(2)}, u32[]{:S(2)}) %collective-permute-start.9) | collective-permute-done | bytes 262176 | tf_op jit(solution)/shard_map/ppermute | solution.py:17
  86.2 4.6 %collective-permute-start.13 = (bf16[2,256,512]{2,1,0:T(8,128)(2,1)S(1)}, bf16[2,256,512]{2,1,0:T(8,128)(2,1)S(1)}, u32[]{:S(2)}, u32[]{:S(2)}) collective-permute-start(bf16[2,256,512]{2,1,0:T(8,128)(2,1)S(1)} %maximum_select_fusion), channel_id=1, source_target_pairs={{0,1},{1,2},{2,3},{3,4},{4,5},{5,6},{6,7},{7,0},{8,9},{9,10},{10,1... | collective-permute-start | bytes 1572872 | tf_op jit(solution)/shard_map/ppermute | solution.py:17
  90.9 1.9 %collective-permute-start.10 = (bf16[2,256,512]{2,1,0:T(8,128)(2,1)S(1)}, bf16[2,256,512]{2,1,0:T(8,128)(2,1)S(1)}, u32[]{:S(2)}, u32[]{:S(2)}) collective-permute-start(bf16[2,256,512]{2,1,0:T(8,128)(2,1)S(1)} %maximum_select_fusion), channel_id=1, source_target_pairs={{0,7},{1,0},{2,1},{3,2},{4,3},{5,4},{6,5},{7,6},{8,15},{9,8},{10,9... | collective-permute-start | bytes 1572872 | tf_op jit(solution)/shard_map/ppermute | solution.py:17
  92.8 5.5 %collective-permute-done.13 = bf16[2,256,512]{2,1,0:T(8,128)(2,1)S(1)} collective-permute-done((bf16[2,256,512]{2,1,0:T(8,128)(2,1)S(1)}, bf16[2,256,512]{2,1,0:T(8,128)(2,1)S(1)}, u32[]{:S(2)}, u32[]{:S(2)}) %collective-permute-start.13) | collective-permute-done | bytes 524320 | tf_op jit(solution)/shard_map/ppermute | solution.py:17
  98.3 5.1 %collective-permute-start.14 = (bf16[2,256,512]{2,1,0:T(8,128)(2,1)S(1)}, bf16[2,256,512]{2,1,0:T(8,128)(2,1)S(1)}, u32[]{:S(2)}, u32[]{:S(2)}) collective-permute-start(bf16[2,256,512]{2,1,0:T(8,128)(2,1)S(1)} %collective-permute-done.13), channel_id=1, source_target_pairs={{0,1},{1,2},{2,3},{3,4},{4,5},{5,6},{6,7},{7,0},{8,9},{9,10},{10,1... | collective-permute-start | bytes 1572872 | tf_op jit(solution)/shard_map/ppermute | solution.py:17
  105.6 5.9 %collective-permute-done.14 = bf16[2,256,512]{2,1,0:T(8,128)(2,1)S(1)} collective-permute-done((bf16[2,256,512]{2,1,0:T(8,128)(2,1)S(1)}, bf16[2,256,512]{2,1,0:T(8,128)(2,1)S(1)}, u32[]{:S(2)}, u32[]{:S(2)}) %collective-permute-start.14) | collective-permute-done | bytes 524320 | tf_op jit(solution)/shard_map/ppermute | solution.py:17
  111.6 5.6 %collective-permute-start.15 = (bf16[2,256,512]{2,1,0:T(8,128)(2,1)S(1)}, bf16[2,256,512]{2,1,0:T(8,128)(2,1)}, u32[]{:S(2)}, u32[]{:S(2)}) collective-permute-start(bf16[2,256,512]{2,1,0:T(8,128)(2,1)S(1)} %collective-permute-done.14), channel_id=1, source_target_pairs={{0,1},{1,2},{2,3},{3,4},{4,5},{5,6},{6,7},{7,0},{8,9},{9,10},{10,1... | collective-permute-start | bytes 1572872 | tf_op jit(solution)/shard_map/ppermute | solution.py:17
  119.6 6.5 %collective-permute-done.15 = bf16[2,256,512]{2,1,0:T(8,128)(2,1)} collective-permute-done((bf16[2,256,512]{2,1,0:T(8,128)(2,1)S(1)}, bf16[2,256,512]{2,1,0:T(8,128)(2,1)}, u32[]{:S(2)}, u32[]{:S(2)}) %collective-permute-start.15) | collective-permute-done | bytes 524320 | tf_op jit(solution)/shard_map/ppermute | solution.py:17
  126.1 5.9 %collective-permute-start.16 = (bf16[2,256,512]{2,1,0:T(8,128)(2,1)}, bf16[2,256,512]{2,1,0:T(8,128)(2,1)S(1)}, u32[]{:S(2)}, u32[]{:S(2)}) collective-permute-start(bf16[2,256,512]{2,1,0:T(8,128)(2,1)} %collective-permute-done.15), channel_id=1, source_target_pairs={{0,1},{1,2},{2,3},{3,4},{4,5},{5,6},{6,7},{7,0},{8,9},{9,10},{10,1... | collective-permute-start | bytes 1572872 | tf_op jit(solution)/shard_map/ppermute | solution.py:17
  132.0 5.7 %fusion = bf16[2,8,512,512]{3,2,1,0:T(8,128)(2,1)S(1)} fusion(s32[]{:T(128)S(6)} %select_n.36, bf16[2,8,512,512]{3,2,1,0:T(8,128)(2,1)} %bitcast.114), kind=kLoop, calls=%fused_computation.2 | loop fusion | flops 4194304 | bytes 16777220 | tf_op jit(solution)/shard_map/jit(_roll_dynamic)/concatenate | solution.py:109
  (54 shorter events, 24.9 us)
Async XLA Ops:
  6.5 33.1 %copy-start = (f32[16,512]{1,0:T(8,128)S(1)}, f32[16,512]{1,0:T(8,128)}, u32[]{:S(2)}) copy-start(f32[16,512]{1,0:T(8,128)} %param.8) | copy-start | bytes 98308
  6.5 125.5 %all-gather.2.cloned.1.call-start = ((), (), s32[]{:S(2)}) async-start(), calls=%async_computation | async-start | bytes 8650752 | tf_op jit(solution)/shard_map/all_gather | solution.py:104
  8.0 12.0 %collective-permute-start = (bf16[3,2,512]{2,1,0:T(2,128)(2,1)S(1)}, bf16[3,2,512]{2,1,0:T(2,128)(2,1)S(1)}, u32[]{:S(2)}, u32[]{:S(2)}) collective-permute-start(bf16[3,2,512]{2,1,0:T(2,128)(2,1)S(1)} %slice.55), channel_id=1, source_target_pairs={{0,16},{16,32},{32,48},{48,64},{64,80},{80,96},{96,112},{112,128},... | collective-permute-start | bytes 18440 | tf_op jit(solution)/shard_map/ppermute | solution.py:13
  21.8 41.7 %copy-start.1 = (f32[16,512]{1,0:T(8,128)S(1)}, f32[16,512]{1,0:T(8,128)}, u32[]{:S(2)}) copy-start(f32[16,512]{1,0:T(8,128)} %param.9) | copy-start | bytes 98308
  23.4 11.7 %collective-permute-start.1 = (f32[16,512]{1,0:T(8,128)S(1)}, f32[16,512]{1,0:T(8,128)S(1)}, u32[]{:S(2)}, u32[]{:S(2)}) collective-permute-start(f32[16,512]{1,0:T(8,128)S(1)} %multiply_reduce_fusion.1), channel_id=1, source_target_pairs={{0,16},{16,32},{32,48},{48,64},{64,80},{80,96},{96,112},{112,128},... | collective-permute-start | bytes 98312 | tf_op jit(solution)/shard_map/ppermute | solution.py:13
  25.3 9.8 %collective-permute-start.2 = (f32[16,512]{1,0:T(8,128)S(1)}, f32[16,512]{1,0:T(8,128)S(1)}, u32[]{:S(2)}, u32[]{:S(2)}) collective-permute-start(f32[16,512]{1,0:T(8,128)S(1)} %multiply_reduce_fusion.1), channel_id=1, source_target_pairs={{0,32},{16,48},{32,64},{48,80},{64,96},{80,112},{96,128},{112,144}... | collective-permute-start | bytes 98312 | tf_op jit(solution)/shard_map/ppermute | solution.py:13
  27.3 9.5 %collective-permute-start.3 = (f32[16,512]{1,0:T(8,128)S(1)}, f32[16,512]{1,0:T(8,128)S(1)}, u32[]{:S(2)}, u32[]{:S(2)}) collective-permute-start(f32[16,512]{1,0:T(8,128)S(1)} %multiply_reduce_fusion.1), channel_id=1, source_target_pairs={{0,48},{16,64},{32,80},{48,96},{64,112},{80,128},{96,144},{112,160... | collective-permute-start | bytes 98312 | tf_op jit(solution)/shard_map/ppermute | solution.py:13
  29.2 10.4 %collective-permute-start.4 = (f32[16,512]{1,0:T(8,128)S(1)}, f32[16,512]{1,0:T(8,128)S(1)}, u32[]{:S(2)}, u32[]{:S(2)}) collective-permute-start(f32[16,512]{1,0:T(8,128)S(1)} %multiply_reduce_fusion.1), channel_id=1, source_target_pairs={{0,64},{16,80},{32,96},{48,112},{64,128},{80,144},{96,160},{112,17... | collective-permute-start | bytes 98312 | tf_op jit(solution)/shard_map/ppermute | solution.py:13
  39.7 10.5 %collective-permute-start.5 = (f32[16,512]{1,0:T(8,128)S(1)}, f32[16,512]{1,0:T(8,128)S(1)}, u32[]{:S(2)}, u32[]{:S(2)}) collective-permute-start(f32[16,512]{1,0:T(8,128)S(1)} %multiply_add_fusion.1), channel_id=1, source_target_pairs={{0,64},{16,80},{32,96},{48,112},{64,128},{80,144},{96,160},{112,17... | collective-permute-start | bytes 98312 | tf_op jit(solution)/shard_map/ppermute | solution.py:13
  42.5 11.4 %collective-permute-start.6 = (f32[16,512]{1,0:T(8,128)S(1)}, f32[16,512]{1,0:T(8,128)S(1)}, u32[]{:S(2)}, u32[]{:S(2)}) collective-permute-start(f32[16,512]{1,0:T(8,128)S(1)} %multiply_add_fusion.1), channel_id=1, source_target_pairs={{0,128},{16,144},{32,160},{48,176},{64,192},{80,208},{96,224},{112... | collective-permute-start | bytes 98312 | tf_op jit(solution)/shard_map/ppermute | solution.py:13
  48.3 9.0 %collective-permute-start.7 = (f32[16,512]{1,0:T(8,128)S(1)}, f32[16,512]{1,0:T(8,128)S(1)}, u32[]{:S(2)}, u32[]{:S(2)}) collective-permute-start(f32[16,512]{1,0:T(8,128)S(1)} %multiply_add_fusion.1), channel_id=1, source_target_pairs={{0,192},{16,208},{32,224},{48,240},{64,256},{80,272},{96,288},{112... | collective-permute-start | bytes 98312 | tf_op jit(solution)/shard_map/ppermute | solution.py:13
  57.3 6.3 %collective-permute-start.8 = (f32[16,512]{1,0:T(8,128)S(1)}, f32[16,512]{1,0:T(8,128)S(1)}, u32[]{:S(2)}, u32[]{:S(2)}) collective-permute-start(f32[16,512]{1,0:T(8,128)S(1)} %multiply_add_fusion), channel_id=1, source_target_pairs={{0,256},{16,272},{32,288},{48,304},{64,320},{80,336},{96,352},{112... | collective-permute-start | bytes 98312 | tf_op jit(solution)/shard_map/ppermute | solution.py:13
  60.1 9.3 %copy-start.2 = (f32[512]{0:T(512)S(1)}, f32[512]{0:T(512)}, u32[]{:S(2)}) copy-start(f32[512]{0:T(512)} %param.10) | copy-start | bytes 6148
  69.7 16.4 %collective-permute-start.9 = (bf16[256,512]{1,0:T(8,128)(2,1)S(1)}, bf16[256,512]{1,0:T(8,128)(2,1)S(1)}, u32[]{:S(2)}, u32[]{:S(2)}) collective-permute-start(bf16[256,512]{1,0:T(8,128)(2,1)S(1)} %fusion.11), channel_id=1, source_target_pairs={{0,8},{1,9},{2,10},{3,11},{4,12},{5,13},{6,14},{7,15},{8,0},{9,1},... | collective-permute-start | bytes 786440 | tf_op jit(solution)/shard_map/ppermute | solution.py:17
  86.2 12.1 %collective-permute-start.13 = (bf16[2,256,512]{2,1,0:T(8,128)(2,1)S(1)}, bf16[2,256,512]{2,1,0:T(8,128)(2,1)S(1)}, u32[]{:S(2)}, u32[]{:S(2)}) collective-permute-start(bf16[2,256,512]{2,1,0:T(8,128)(2,1)S(1)} %maximum_select_fusion), channel_id=1, source_target_pairs={{0,1},{1,2},{2,3},{3,4},{4,5},{5,6},{6,7},{7,0},{8,9},{9,10},{10,1... | collective-permute-start | bytes 1572872 | tf_op jit(solution)/shard_map/ppermute | solution.py:17
  90.9 12.9 %collective-permute-start.10 = (bf16[2,256,512]{2,1,0:T(8,128)(2,1)S(1)}, bf16[2,256,512]{2,1,0:T(8,128)(2,1)S(1)}, u32[]{:S(2)}, u32[]{:S(2)}) collective-permute-start(bf16[2,256,512]{2,1,0:T(8,128)(2,1)S(1)} %maximum_select_fusion), channel_id=1, source_target_pairs={{0,7},{1,0},{2,1},{3,2},{4,3},{5,4},{6,5},{7,6},{8,15},{9,8},{10,9... | collective-permute-start | bytes 1572872 | tf_op jit(solution)/shard_map/ppermute | solution.py:17
  98.3 13.3 %collective-permute-start.14 = (bf16[2,256,512]{2,1,0:T(8,128)(2,1)S(1)}, bf16[2,256,512]{2,1,0:T(8,128)(2,1)S(1)}, u32[]{:S(2)}, u32[]{:S(2)}) collective-permute-start(bf16[2,256,512]{2,1,0:T(8,128)(2,1)S(1)} %collective-permute-done.13), channel_id=1, source_target_pairs={{0,1},{1,2},{2,3},{3,4},{4,5},{5,6},{6,7},{7,0},{8,9},{9,10},{10,1... | collective-permute-start | bytes 1572872 | tf_op jit(solution)/shard_map/ppermute | solution.py:17
  103.7 13.5 %copy-start.3 = (bf16[2,256,512]{2,1,0:T(8,128)(2,1)}, bf16[2,256,512]{2,1,0:T(8,128)(2,1)S(1)}, u32[]{:S(2)}) copy-start(bf16[2,256,512]{2,1,0:T(8,128)(2,1)S(1)} %collective-permute-done.10) | copy-start | bytes 1572868
  103.7 14.0 %collective-permute-start.11 = (bf16[2,256,512]{2,1,0:T(8,128)(2,1)S(1)}, bf16[2,256,512]{2,1,0:T(8,128)(2,1)S(1)}, u32[]{:S(2)}, u32[]{:S(2)}) collective-permute-start(bf16[2,256,512]{2,1,0:T(8,128)(2,1)S(1)} %collective-permute-done.10), channel_id=1, source_target_pairs={{0,7},{1,0},{2,1},{3,2},{4,3},{5,4},{6,5},{7,6},{8,15},{9,8},{10,9... | collective-permute-start | bytes 1572872 | tf_op jit(solution)/shard_map/ppermute | solution.py:17
  111.6 14.6 %collective-permute-start.15 = (bf16[2,256,512]{2,1,0:T(8,128)(2,1)S(1)}, bf16[2,256,512]{2,1,0:T(8,128)(2,1)}, u32[]{:S(2)}, u32[]{:S(2)}) collective-permute-start(bf16[2,256,512]{2,1,0:T(8,128)(2,1)S(1)} %collective-permute-done.14), channel_id=1, source_target_pairs={{0,1},{1,2},{2,3},{3,4},{4,5},{5,6},{6,7},{7,0},{8,9},{9,10},{10,1... | collective-permute-start | bytes 1572872 | tf_op jit(solution)/shard_map/ppermute | solution.py:17
  117.7 23.7 %collective-permute-start.12 = (bf16[2,256,512]{2,1,0:T(8,128)(2,1)S(1)}, bf16[2,256,512]{2,1,0:T(8,128)(2,1)S(1)}, u32[]{:S(2)}, u32[]{:S(2)}) collective-permute-start(bf16[2,256,512]{2,1,0:T(8,128)(2,1)S(1)} %collective-permute-done.11), channel_id=1, source_target_pairs={{0,7},{1,0},{2,1},{3,2},{4,3},{5,4},{6,5},{7,6},{8,15},{9,8},{10,9... | collective-permute-start | bytes 1572872 | tf_op jit(solution)/shard_map/ppermute | solution.py:17
  126.1 15.7 %collective-permute-start.16 = (bf16[2,256,512]{2,1,0:T(8,128)(2,1)}, bf16[2,256,512]{2,1,0:T(8,128)(2,1)S(1)}, u32[]{:S(2)}, u32[]{:S(2)}) collective-permute-start(bf16[2,256,512]{2,1,0:T(8,128)(2,1)} %collective-permute-done.15), channel_id=1, source_target_pairs={{0,1},{1,2},{2,3},{3,4},{4,5},{5,6},{6,7},{7,0},{8,9},{9,10},{10,1... | collective-permute-start | bytes 1572872 | tf_op jit(solution)/shard_map/ppermute | solution.py:17
  132.0 5.7 %copy-start.4 = (bf16[2,256,512]{2,1,0:T(8,128)(2,1)S(1)}, bf16[2,256,512]{2,1,0:T(8,128)(2,1)}, u32[]{:S(2)}) copy-start(bf16[2,256,512]{2,1,0:T(8,128)(2,1)} %copy-done.3) | copy-start | bytes 1572868
Sparse Core Ops, SparseCore 0:
  9.5 84.2 all-gather.1
